TPU v7x, 512 devices: a whole 4x8x8 slice. The times are simulated.
512 devices in a mesh: table: 64 (over y, z), expert: 8 (over x, core).
Axes of the slice: x: 4, y: 8, z: 8, core: 2. Of those that a mesh axis runs over, the one named last changes fastest.
Arguments:
- table: bfloat16 [64, 512, 256], P('table'), may hold values from -127 to 127, as said below
- row_scale: float32 [64, 512], P('table'), may hold values from 0.3 to 3
- windows: int32 [64, 8, 256], P('table', 'expert'), may hold values from 0 to 511, as said below
- bag_idx: int32 [64, 8, 8192, 8], P('table', 'expert'), may hold values from 0 to 255
- bag_len: int32 [64, 8, 8192], P('table', 'expert'), may hold values from 1 to 8
- feat_gain: float32 [64, 256], replicated, may hold values from 0.03 to 0.3
- norm_gain: float32 [256], replicated, may hold values from 0.5 to 1.5
- expert_ids: int32 [8, 8192, 1], P('expert', 'table'), may hold values from 0 to 63; in each aligned block of 128 rows (0 to 127, 128 to 255, ..., all dimensions but the last counted through in order) at most 4 rows name the same one
- w_in: bfloat16 [64, 256, 4096], P('table', None, 'expert'), may hold values from -0.375 to 0.375
- w_out: bfloat16 [64, 4096, 256], P('table', 'expert'), may hold values from -0.09375 to 0.09375
- w_tow1: bfloat16 [3, 256, 256], replicated, may hold values from -0.375 to 0.375
- w_tow2: float32 [3, 256], replicated, may hold values from -1.5 to 1.5
- targets: float32 [8, 8192, 3], P('expert', 'table'), may hold values from 0 to 1
Outputs:
- predictions: float32 [8, 8192, 3], P('expert', 'table')
- grad_table: float32 [64, 512, 256], P('table', 'expert')
- grad_w_in: float32 [64, 256, 4096], P('table', None, 'expert')
- grad_w_out: float32 [64, 4096, 256], P('table', 'expert')
Inputs may be any that keep to these rules, and one draw needn't show every extreme that they name: `table`: every entry is an integer. Each row windows[f, g] holds 256 distinct row numbers of feature f's table. `expert_ids`: in each aligned block of 128 samples (the samples of one device) no expert is named by more than 4 samples.
All inputs are finite; a program needn't handle non-finite values.
Results may differ from a plain program's by a relative error of at most 0.02.
Values may be sent and summed in bfloat16 or wider, within the bound.
No kernel may reach another device: no remote copies, remote signals or barrier semaphores. Data moves between devices by JAX's collectives and lax.ppermute only.
A program may use at most 128 MiB of HBM per device.

v0:
```python
import math

import jax
import jax.numpy as jnp
from jax import lax
from jax.sharding import PartitionSpec as P

code_range = 127.0


def silu_slope(values):
    sigma = jax.nn.sigmoid(values)
    return sigma * (1.0 + values * (1.0 - sigma))


def bag_counts(indices, lengths, window):
    total = indices.shape[0]
    block = math.gcd(total, 512)
    positions = jnp.arange(window, dtype=jnp.int32)
    slots = jnp.arange(indices.shape[1], dtype=jnp.int32)

    def count_block(operands):
        block_idx, block_len = operands
        live = (slots[None, :] < block_len[:, None]).astype(jnp.float32)
        hits = (block_idx[:, :, None] == positions[None, None, :]).astype(jnp.float32)
        return jnp.sum(hits * live[:, :, None], axis=1).astype(jnp.bfloat16)

    blocked = lax.map(
        count_block,
        (
            indices.reshape(total // block, block, indices.shape[1]),
            lengths.reshape(total // block, block),
        ),
    )
    return blocked.reshape(total, window)


def dispatch(buffer):
    arrived = lax.all_to_all(buffer, "table", split_axis=0, concat_axis=0, tiled=True)
    columns = lax.all_gather(arrived[None], "expert", axis=0, tiled=True)
    return columns.reshape(-1, buffer.shape[-1])


def column_sum(term_fn, local_rows):
    return lax.psum_scatter(
        term_fn(jnp.int32(0), lax.axis_size("expert") * local_rows).astype(jnp.bfloat16),
        "expert",
        scatter_dimension=0,
        tiled=True,
    ).astype(jnp.float32)


def send_back(result, experts, capacity):
    rows_back = result.astype(jnp.bfloat16).reshape(experts, capacity, result.shape[-1])
    arrived = lax.all_to_all(rows_back, "table", split_axis=0, concat_axis=0, tiled=True)
    return arrived.reshape(experts * capacity, result.shape[-1])


def local(
    table,
    row_scale,
    windows,
    bag_idx,
    bag_len,
    feat_gain,
    norm_gain,
    expert_ids,
    w_in,
    w_out,
    w_tow1,
    w_tow2,
    targets,
):
    owners = lax.axis_size("table")
    samples = expert_ids.shape[1]
    capacity = max(2, 2 * samples // owners)
    local_rows = owners * capacity
    contract_rows = (((0,), (0,)), ((), ()))
    contract_cols = (((1,), (1,)), ((), ()))
    window = windows[0, 0]
    picked = jnp.take(table[0], window, axis=0).astype(jnp.float32)
    scales = jnp.take(row_scale[0], window)
    dequant = (picked * scales[:, None] / code_range).astype(jnp.bfloat16)
    counts = bag_counts(bag_idx[0, 0], bag_len[0, 0], window.shape[0])
    pooled = jnp.dot(counts, dequant, preferred_element_type=jnp.float32).astype(jnp.bfloat16)
    features = lax.all_to_all(
        pooled.reshape(owners, samples, pooled.shape[-1]),
        "table",
        split_axis=0,
        concat_axis=0,
        tiled=True,
    )
    summed = jnp.sum(features.astype(jnp.float32) * feat_gain[:, None, :], axis=0)
    inverse = lax.rsqrt(jnp.mean(summed * summed, axis=-1, keepdims=True) + 1e-05)
    normed = (summed * inverse * norm_gain).astype(jnp.bfloat16)
    chosen = expert_ids[0, :, 0]
    member = (chosen[:, None] == jnp.arange(owners, dtype=jnp.int32)[None, :]).astype(jnp.int32)
    ranks = jnp.cumsum(member, axis=0) - member
    slot_of = jnp.sum(ranks * member, axis=1)
    target_slot = chosen * capacity + slot_of
    placing = (jnp.arange(local_rows, dtype=jnp.int32)[:, None] == target_slot[None, :]).astype(
        jnp.bfloat16
    )
    outgoing = jnp.dot(placing, normed, preferred_element_type=jnp.float32).astype(jnp.bfloat16)
    gathered = dispatch(outgoing.reshape(owners, capacity, outgoing.shape[-1]))
    weight_in = w_in[0]
    weight_out = w_out[0]
    pre_act = jnp.dot(gathered, weight_in, preferred_element_type=jnp.float32)
    hidden = jax.nn.silu(pre_act).astype(jnp.bfloat16)

    def forward_term(start, count):
        return jnp.dot(hidden, weight_out, preferred_element_type=jnp.float32)

    expert_out = send_back(column_sum(forward_term, local_rows), owners, capacity)
    mixture = lax.dot_general(
        placing, expert_out, contract_rows, preferred_element_type=jnp.float32
    )
    joined = (normed.astype(jnp.float32) + mixture).astype(jnp.bfloat16)
    tower_pre = jnp.einsum("be,kem->kbm", joined, w_tow1, preferred_element_type=jnp.float32)
    logits = jnp.sum(jax.nn.silu(tower_pre) * w_tow2[:, None, :], axis=-1)
    predicted = jnp.stack(
        [jax.nn.sigmoid(logits[0]), jax.nn.sigmoid(logits[1]), logits[2]], axis=-1
    )
    logit_grad = predicted - targets[0]
    tower_grad = (logit_grad.T[:, :, None] * w_tow2[:, None, :] * silu_slope(tower_pre)).astype(
        jnp.bfloat16
    )
    joined_grad = jnp.einsum(
        "kbm,kem->be", tower_grad, w_tow1, preferred_element_type=jnp.float32
    ).astype(jnp.bfloat16)
    back_rows = jnp.dot(placing, joined_grad, preferred_element_type=jnp.float32).astype(
        jnp.bfloat16
    )
    gathered_grad = dispatch(back_rows.reshape(owners, capacity, back_rows.shape[-1]))
    grad_hidden = lax.dot_general(
        gathered_grad, weight_out, contract_cols, preferred_element_type=jnp.float32
    )
    grad_pre = (grad_hidden * silu_slope(pre_act)).astype(jnp.bfloat16)
    grad_out = lax.dot_general(
        hidden, gathered_grad, contract_rows, preferred_element_type=jnp.float32
    )
    grad_in = lax.dot_general(gathered, grad_pre, contract_rows, preferred_element_type=jnp.float32)

    def backward_term(start, count):
        return lax.dot_general(
            grad_pre, weight_in, contract_cols, preferred_element_type=jnp.float32
        )

    input_grad = send_back(column_sum(backward_term, local_rows), owners, capacity)
    mixture_grad = lax.dot_general(
        placing, input_grad, contract_rows, preferred_element_type=jnp.float32
    )
    normed_grad = joined_grad.astype(jnp.float32) + mixture_grad
    scaled_grad = normed_grad * norm_gain
    summed_grad = inverse * (
        scaled_grad
        - summed * inverse * inverse * jnp.mean(scaled_grad * summed, axis=-1, keepdims=True)
    )
    feature_grad = (summed_grad[None, :, :] * feat_gain[:, None, :]).astype(jnp.bfloat16)
    returned = lax.all_to_all(
        feature_grad, "table", split_axis=0, concat_axis=0, tiled=True
    ).reshape(owners * samples, feature_grad.shape[-1])
    window_grad = lax.dot_general(
        counts, returned, contract_rows, preferred_element_type=jnp.float32
    )
    row_select = (jnp.arange(table.shape[1], dtype=jnp.int32)[:, None] == window[None, :]).astype(
        jnp.float32
    )
    row_grad = jnp.dot(row_select, window_grad, precision=lax.Precision.HIGHEST)
    table_grad = lax.psum_scatter(
        row_grad.astype(jnp.bfloat16), "expert", scatter_dimension=0, tiled=True
    ).astype(jnp.float32)
    return (predicted[None], table_grad[None], grad_in[None], grad_out[None])


def solution(mesh):
    in_specs = (
        P("table", None, None),
        P("table", None),
        P("table", "expert", None),
        P("table", "expert", None, None),
        P("table", "expert", None),
        P(),
        P(),
        P("expert", "table", None),
        P("table", None, "expert"),
        P("table", "expert", None),
        P(),
        P(),
        P("expert", "table", None),
    )
    out_specs = (
        P("expert", "table", None),
        P("table", "expert", None),
        P("table", None, "expert"),
        P("table", "expert", None),
    )
    return jax.shard_map(local, mesh=mesh, in_specs=in_specs, out_specs=out_specs, check_vma=False)
```

profile of v0, /device:TPU:40, one launch (start us, length us, event | category | flops | bytes accessed | tf_op | source)
XLA Modules:
  0.0 661.0 jit_solution(6694098426931538434)
XLA Ops:
  10.0 75.1 %while.11 = (s32[]{:T(128)}, bf16[16,512,256]{2,1,0:T(8,128)(2,1)}, s32[16,512,8]{1,2,0:T(8,128)}, s32[16,512]{1,0:T(8,128)S(1)}, s32[]{:T(128)}) while((s32[]{:T(128)}, bf16[16,512,256]{2,1,0:T(8,128)(2,1)}, s32[16,512,8]{1,2,0:T(8,128)}, s32[16,512]{1,0:T(8,128)S(1)}, s32[]{:T(128)}) %tuple.50), condition=%wide.region_2.3_spmd.clone, body=%wide.region_0.0_spmd.clone.sunk | while | flops 3022850 | bytes 940613 | solution.py:28
  11.0 3.0 select_reduce_fusion.3
  15.7 3.0 select_reduce_fusion.3
  20.4 3.0 select_reduce_fusion.3
  29.8 3.0 select_reduce_fusion.3
  39.2 3.0 select_reduce_fusion.3
  43.9 3.0 select_reduce_fusion.3
  48.5 3.0 select_reduce_fusion.3
  53.2 3.0 select_reduce_fusion.3
  76.6 3.0 select_reduce_fusion.3
  81.3 3.0 select_reduce_fusion.3
  88.2 5.5 convolution_convert_fusion
  93.7 16.6 %all-to-all-start = ((bf16[64,128,256]{2,1,0:T(8,128)(2,1)}), bf16[64,128,256]{2,1,0:T(8,128)(2,1)}, u32[]{:S(2)}, u32[]{:S(2)}) async-start(bf16[64,128,256]{2,1,0:T(8,128)(2,1)} %bitcast.88), calls=%async_computation | async-start | bytes 8388608 | tf_op jit(solution)/shard_map/all_to_all | solution.py:86
  110.9 115.2 %all-to-all-done = bf16[64,128,256]{2,1,0:T(8,128)(2,1)} async-done(((bf16[64,128,256]{2,1,0:T(8,128)(2,1)}), bf16[64,128,256]{2,1,0:T(8,128)(2,1)}, u32[]{:S(2)}, u32[]{:S(2)}) %all-to-all-start) | async-done | bytes 4194336 | tf_op jit(solution)/shard_map/all_to_all | solution.py:86
  226.1 3.1 multiply_reduce_fusion
  229.6 34.9 %all_to_all.30 = bf16[64,4,256]{2,1,0:T(4,128)(2,1)} all-to-all(bf16[64,4,256]{2,1,0:T(4,128)(2,1)S(1)} %reshape.210), channel_id=1, replica_groups=mesh['table'=64,'expert'=8] {'table'}, dimensions={0} | all-to-all | bytes 262144 | tf_op jit(solution)/shard_map/all_to_all | solution.py:39
  264.6 23.8 %all-gather.5.cloned.1.call-done = bf16[512,4,256]{2,1,0:T(4,128)(2,1)} async-done(((bf16[64,4,256]{2,1,0:T(4,128)(2,1)}), bf16[512,4,256]{2,1,0:T(4,128)(2,1)}) %all-gather.5.cloned.1.call-update) | async-done | bytes 1048592 | tf_op jit(solution)/shard_map/all_gather | solution.py:40
  289.8 3.1 multiply_convert_fusion.2
  296.1 37.5 %reduce-scatter.4.cloned.1.call-done = bf16[256,256]{1,0:T(8,128)(2,1)} async-done(((bf16[2048,256]{1,0:T(8,128)(2,1)}), bf16[256,256]{1,0:T(8,128)(2,1)}) %reduce-scatter.4.cloned.1.call-update) | async-done | bytes 131088 | tf_op jit(solution)/shard_map/reduce_scatter | solution.py:45
  334.6 21.9 %all_to_all.31 = bf16[64,4,256]{2,1,0:T(4,128)(2,1)S(1)} all-to-all(bf16[64,4,256]{2,1,0:T(4,128)(2,1)S(1)} %reshape.212), channel_id=1, replica_groups=mesh['table'=64,'expert'=8] {'table'}, dimensions={0} | all-to-all | bytes 262144 | tf_op jit(solution)/shard_map/all_to_all | solution.py:55
  357.6 17.2 %all_to_all.32 = bf16[64,4,256]{2,1,0:T(4,128)(2,1)} all-to-all(bf16[64,4,256]{2,1,0:T(4,128)(2,1)S(1)} %reshape.214), channel_id=1, replica_groups=mesh['table'=64,'expert'=8] {'table'}, dimensions={0} | all-to-all | bytes 262144 | tf_op jit(solution)/shard_map/all_to_all | solution.py:39
  375.1 21.8 %all-gather.7.cloned.1.call-done = bf16[512,4,256]{2,1,0:T(4,128)(2,1)} async-done(((bf16[64,4,256]{2,1,0:T(4,128)(2,1)}), bf16[512,4,256]{2,1,0:T(4,128)(2,1)}) %all-gather.7.cloned.1.call-update) | async-done | bytes 1048592 | tf_op jit(solution)/shard_map/all_gather | solution.py:40
  398.2 5.2 multiply_convert_fusion.1
  403.5 3.3 convolution_convert_fusion.1
  406.8 37.6 %reduce-scatter.6.cloned.1.call-done = bf16[256,256]{1,0:T(8,128)(2,1)} async-done(((bf16[2048,256]{1,0:T(8,128)(2,1)}), bf16[256,256]{1,0:T(8,128)(2,1)}) %reduce-scatter.6.cloned.1.call-update) | async-done | bytes 131088 | tf_op jit(solution)/shard_map/reduce_scatter | solution.py:45
  445.3 22.0 %all_to_all.33 = bf16[64,4,256]{2,1,0:T(4,128)(2,1)S(1)} all-to-all(bf16[64,4,256]{2,1,0:T(4,128)(2,1)S(1)} %reshape.216), channel_id=1, replica_groups=mesh['table'=64,'expert'=8] {'table'}, dimensions={0} | all-to-all | bytes 262144 | tf_op jit(solution)/shard_map/all_to_all | solution.py:55
  467.8 3.4 multiply_convert_fusion
  471.2 9.6 %all-to-all-start.5 = ((bf16[64,128,256]{2,1,0:T(8,128)(2,1)}), bf16[64,128,256]{2,1,0:T(8,128)(2,1)}, u32[]{:S(2)}, u32[]{:S(2)}) async-start(bf16[64,128,256]{2,1,0:T(8,128)(2,1)} %multiply_convert_fusion), calls=%async_computation.7 | async-start | bytes 8388608 | tf_op jit(solution)/shard_map/all_to_all | solution.py:160
  481.4 122.4 %all-to-all-done.5 = bf16[64,128,256]{2,1,0:T(8,128)(2,1)} async-done(((bf16[64,128,256]{2,1,0:T(8,128)(2,1)}), bf16[64,128,256]{2,1,0:T(8,128)(2,1)}, u32[]{:S(2)}, u32[]{:S(2)}) %all-to-all-start.5) | async-done | bytes 4194336 | tf_op jit(solution)/shard_map/all_to_all | solution.py:160
  603.9 4.7 fusion.35
  609.8 3.4 convolution_bitcast_fusion.1
  614.8 38.3 %reduce-scatter.8.cloned.1.call-done = bf16[64,256]{1,0:T(8,128)(2,1)} async-done(((bf16[512,256]{1,0:T(8,128)(2,1)}), bf16[64,256]{1,0:T(8,128)(2,1)}) %reduce-scatter.8.cloned.1.call-update) | async-done | bytes 32784 | tf_op jit(solution)/shard_map/reduce_scatter | solution.py:170
  (177 shorter events, 66.1 us)
Async XLA Ops:
  7.2 349.3 %copy-start = (bf16[3,256,256]{2,1,0:T(8,128)(2,1)S(1)}, bf16[3,256,256]{2,1,0:T(8,128)(2,1)}, u32[]{:S(2)}) copy-start(bf16[3,256,256]{2,1,0:T(8,128)(2,1)} %param.25) | copy-start | bytes 1179652
  9.9 75.1 %copy-start.1 = (f32[1,512]{1,0:T(1,128)S(1)}, f32[1,512]{1,0:T(1,128)}, u32[]{:S(2)}) copy-start(f32[1,512]{1,0:T(1,128)} %param.16) | copy-start | bytes 6148
  9.9 77.1 %copy-start.2 = (bf16[1,512,256]{2,1,0:T(8,128)(2,1)S(1)}, bf16[1,512,256]{2,1,0:T(8,128)(2,1)}, u32[]{:S(2)}) copy-start(bf16[1,512,256]{2,1,0:T(8,128)(2,1)} %param.15) | copy-start | bytes 786436
  10.0 78.2 %copy-start.8 = (s32[1,1,256]{2,1,0:T(1,128)S(1)}, s32[1,1,256]{2,1,0:T(1,128)}, u32[]{:S(2)}) copy-start(s32[1,1,256]{2,1,0:T(1,128)} %param.17) | copy-start | bytes 3076
  93.7 16.7 %copy-start.10 = (s32[1,128,1]{1,2,0:T(1,128)S(1)}, s32[1,128,1]{1,2,0:T(1,128)}, u32[]{:S(2)}) copy-start(s32[1,128,1]{1,2,0:T(1,128)} %param.22) | copy-start | bytes 1540
  93.7 132.4 %copy-start.6 = (f32[64,256]{1,0:T(8,128)S(1)}, f32[64,256]{1,0:T(8,128)}, u32[]{:S(2)}) copy-start(f32[64,256]{1,0:T(8,128)} %param.20) | copy-start | bytes 196612
  93.7 132.4 %all-to-all-start = ((bf16[64,128,256]{2,1,0:T(8,128)(2,1)}), bf16[64,128,256]{2,1,0:T(8,128)(2,1)}, u32[]{:S(2)}, u32[]{:S(2)}) async-start(bf16[64,128,256]{2,1,0:T(8,128)(2,1)} %bitcast.88), calls=%async_computation | async-start | bytes 8388608 | tf_op jit(solution)/shard_map/all_to_all | solution.py:86
  110.3 119.0 %copy-start.9 = (f32[256]{0:T(256)S(1)}, f32[256]{0:T(256)}, u32[]{:S(2)}) copy-start(f32[256]{0:T(256)} %param.21) | copy-start | bytes 3076
  110.3 179.5 %copy-start.7 = (bf16[1,256,512]{2,1,0:T(8,128)(2,1)S(1)}, bf16[1,256,512]{2,1,0:T(8,128)(2,1)}, u32[]{:S(2)}) copy-start(bf16[1,256,512]{2,1,0:T(8,128)(2,1)} %param.23) | copy-start | bytes 786436
  110.4 178.1 %all-gather.5.cloned.1.call-start = ((), (), s32[]{:S(2)}) async-start(), calls=%async_computation.12 | async-start | bytes 1179648 | tf_op jit(solution)/shard_map/all_gather | solution.py:40
  264.6 69.0 %reduce-scatter.4.cloned.1.call-start = ((), (), s32[]{:S(2)}) async-start(), calls=%async_computation.9 | async-start | bytes 1179648 | tf_op jit(solution)/shard_map/reduce_scatter | solution.py:45
  289.8 3.2 copy-start.5
  289.8 4.5 copy-start.12
  293.0 1.3 copy-start.3
  293.0 63.5 %copy-start.13 = (f32[3,256]{1,0:T(4,128)S(1)}, f32[3,256]{1,0:T(4,128)}, u32[]{:S(2)}) copy-start(f32[3,256]{1,0:T(4,128)} %param.26) | copy-start | bytes 9220
  294.3 62.7 %copy-start.11 = (f32[1,128,3]{1,0,2:T(1,128)S(1)}, f32[1,128,3]{1,0,2:T(1,128)}, u32[]{:S(2)}) copy-start(f32[1,128,3]{1,0,2:T(1,128)} %param.27) | copy-start | bytes 4612
  296.0 100.9 %all-gather.7.cloned.1.call-start = ((), (), s32[]{:S(2)}) async-start(), calls=%async_computation.13 | async-start | bytes 1179648 | tf_op jit(solution)/shard_map/all_gather | solution.py:40
  374.8 69.6 %reduce-scatter.6.cloned.1.call-start = ((), (), s32[]{:S(2)}) async-start(), calls=%async_computation.10 | async-start | bytes 1179648 | tf_op jit(solution)/shard_map/reduce_scatter | solution.py:45
  471.2 132.7 %all-to-all-start.5 = ((bf16[64,128,256]{2,1,0:T(8,128)(2,1)}), bf16[64,128,256]{2,1,0:T(8,128)(2,1)}, u32[]{:S(2)}, u32[]{:S(2)}) async-start(bf16[64,128,256]{2,1,0:T(8,128)(2,1)} %multiply_convert_fusion), calls=%async_computation.7 | async-start | bytes 8388608 | tf_op jit(solution)/shard_map/all_to_all | solution.py:160
  480.8 172.2 %reduce-scatter.8.cloned.1.call-start = ((), (), s32[]{:S(2)}) async-start(), calls=%async_computation.11 | async-start | bytes 294912 | tf_op jit(solution)/shard_map/reduce_scatter | solution.py:170
  608.6 4.6 copy-start.4
Sparse Core Ops, SparseCore 0:
  264.7 23.6 all-gather.4
  296.1 37.4 reduce-scatter.3
  374.9 21.9 all-gather.6
  406.9 37.4 reduce-scatter.5
  609.9 43.1 reduce-scatter.7
where the time goes:
time: 663 us; the launch traced here: 661 us
  waiting for transfers between devices  397 us (60%)
  blocking collectives  96 us (14%)
  other arithmetic  58.2 us (9%)
  local copies, waits for them, and re-layouts  37.5 us (6%)
  matrix products  31.3 us (5%)
  starting transfers between devices  26.6 us (4%)
  between operations  14.1 us (2%)
    all_to_all x1, waiting for transfers between devices, local(): lax.all_to_all(feature_grad, 'table', split_axis=0, concat_axis=0, tiled=...  122 us
    all_to_all x1, waiting for transfers between devices, local(): lax.all_to_all(pooled.reshape(owners, samples, pooled.shape[-1]), 'table'...  115 us
    reduce_scatter x2, waiting for transfers between devices, column_sum(): lax.psum_scatter(term_fn(jnp.int32(0), lax.axis_size('expert') * local_ro...  75.1 us
    all_to_all x2, blocking collectives, dispatch(): lax.all_to_all(buffer, 'table', split_axis=0, concat_axis=0, tiled=True)  52.1 us
    reduce_sum x16, other arithmetic, count_block(): return jnp.sum(hits * live[:, :, None], axis=1).astype(jnp.bfloat16)  47.3 us
    all_gather x2, waiting for transfers between devices, dispatch(): columns = lax.all_gather(arrived[None], 'expert', axis=0, tiled=True)  45.6 us
    all_to_all x2, blocking collectives, send_back(): lax.all_to_all(rows_back, 'table', split_axis=0, concat_axis=0, tiled=True)  43.8 us
    reduce_scatter x1, waiting for transfers between devices, local(): lax.psum_scatter(row_grad.astype(jnp.bfloat16), 'expert', scatter_dimensi...  38.3 us
  transfers between devices with their start and end apart: 7, of which 7 were waited for; matrix products, arithmetic and copies ran while one was open for 1% of the time, Pallas kernels for 0%

commit v1 on v0

v1 whole, which is shorter than its diff:
```python
import jax
import jax.numpy as jnp
from jax import lax
from jax.sharding import PartitionSpec as P

code_range = 127.0


def silu_slope(values):
    sigma = jax.nn.sigmoid(values)
    return sigma * (1.0 + values * (1.0 - sigma))


def bag_counts_t(indices, lengths, window):
    slots = jnp.arange(indices.shape[1], dtype=jnp.int32)
    live = jnp.where(slots[:, None] < lengths[None, :], indices.T, -1)
    positions = jnp.arange(window, dtype=jnp.int32)
    hits = (live[:, None, :] == positions[None, :, None]).astype(jnp.float32)
    return jnp.sum(hits, axis=0).astype(jnp.bfloat16)


def to_owners(rows, owners):
    shaped = rows.reshape(owners, rows.shape[0] // owners, rows.shape[-1])
    arrived = lax.all_to_all(shaped, "table", split_axis=0, concat_axis=0, tiled=True)
    return arrived.reshape(rows.shape)


def shard_partials(left, right, shards):
    rows, width = left.shape
    split_left = left.reshape(rows, shards, width // shards)
    split_right = right.reshape(shards, width // shards, right.shape[-1])
    partials = jnp.einsum("rkf,kfe->kre", split_left, split_right, preferred_element_type=jnp.float32)
    return jnp.sum(partials.astype(jnp.bfloat16).astype(jnp.float32), axis=0).astype(jnp.bfloat16)


def local(
    table,
    row_scale,
    windows,
    bag_idx,
    bag_len,
    feat_gain,
    norm_gain,
    expert_ids,
    w_in,
    w_out,
    w_tow1,
    w_tow2,
    targets,
):
    owners = lax.axis_size("table")
    samples = expert_ids.shape[1]
    capacity = max(2, 2 * samples // owners)
    local_rows = owners * capacity
    contract_rows = (((0,), (0,)), ((), ()))
    contract_cols = (((1,), (1,)), ((), ()))
    weight_in = w_in[0]
    weight_out = w_out[0]
    full_in = lax.all_gather(weight_in, "expert", axis=1, tiled=True)
    full_out = lax.all_gather(weight_out, "expert", axis=0, tiled=True)
    shards = full_in.shape[1] // weight_in.shape[1]

    window = windows[0, 0]
    picked = jnp.take(table[0], window, axis=0).astype(jnp.float32)
    scales = jnp.take(row_scale[0], window)
    dequant = (picked * scales[:, None] / code_range).astype(jnp.bfloat16)
    counts_t = bag_counts_t(bag_idx[0, 0], bag_len[0, 0], window.shape[0])
    pooled = lax.dot_general(
        counts_t, dequant, contract_rows, preferred_element_type=jnp.float32
    ).astype(jnp.bfloat16)
    features = lax.all_to_all(
        pooled.reshape(owners, samples, pooled.shape[-1]),
        "table",
        split_axis=0,
        concat_axis=0,
        tiled=True,
    )
    summed = jnp.sum(features.astype(jnp.float32) * feat_gain[:, None, :], axis=0)
    inverse = lax.rsqrt(jnp.mean(summed * summed, axis=-1, keepdims=True) + 1e-05)
    normed = (summed * inverse * norm_gain).astype(jnp.bfloat16)

    chosen = expert_ids[0, :, 0]
    member = (chosen[:, None] == jnp.arange(owners, dtype=jnp.int32)[None, :]).astype(jnp.int32)
    ranks = jnp.cumsum(member, axis=0) - member
    slot_of = jnp.sum(ranks * member, axis=1)
    target_slot = chosen * capacity + slot_of
    placing = (jnp.arange(local_rows, dtype=jnp.int32)[:, None] == target_slot[None, :]).astype(
        jnp.bfloat16
    )
    outgoing = jnp.dot(placing, normed, preferred_element_type=jnp.float32).astype(jnp.bfloat16)
    rows = to_owners(outgoing, owners)
    pre_act = jnp.dot(rows, full_in, preferred_element_type=jnp.float32)
    hidden = jax.nn.silu(pre_act).astype(jnp.bfloat16)
    expert_out = to_owners(shard_partials(hidden, full_out, shards), owners)
    mixture = lax.dot_general(
        placing, expert_out, contract_rows, preferred_element_type=jnp.float32
    )
    joined = (normed.astype(jnp.float32) + mixture).astype(jnp.bfloat16)
    tower_pre = jnp.einsum("be,kem->kbm", joined, w_tow1, preferred_element_type=jnp.float32)
    logits = jnp.sum(jax.nn.silu(tower_pre) * w_tow2[:, None, :], axis=-1)
    predicted = jnp.stack(
        [jax.nn.sigmoid(logits[0]), jax.nn.sigmoid(logits[1]), logits[2]], axis=-1
    )
    logit_grad = predicted - targets[0]
    tower_grad = (logit_grad.T[:, :, None] * w_tow2[:, None, :] * silu_slope(tower_pre)).astype(
        jnp.bfloat16
    )
    joined_grad = jnp.einsum(
        "kbm,kem->be", tower_grad, w_tow1, preferred_element_type=jnp.float32
    ).astype(jnp.bfloat16)
    back_rows = jnp.dot(placing, joined_grad, preferred_element_type=jnp.float32).astype(
        jnp.bfloat16
    )
    row_grads = to_owners(back_rows, owners)
    grad_hidden = lax.dot_general(
        row_grads, full_out, contract_cols, preferred_element_type=jnp.float32
    )
    grad_pre = (grad_hidden * silu_slope(pre_act)).astype(jnp.bfloat16)
    input_grad = to_owners(shard_partials(grad_pre, full_in.T, shards), owners)
    mixture_grad = lax.dot_general(
        placing, input_grad, contract_rows, preferred_element_type=jnp.float32
    )
    normed_grad = joined_grad.astype(jnp.float32) + mixture_grad
    scaled_grad = normed_grad * norm_gain
    summed_grad = inverse * (
        scaled_grad
        - summed * inverse * inverse * jnp.mean(scaled_grad * summed, axis=-1, keepdims=True)
    )
    feature_grad = (summed_grad[None, :, :] * feat_gain[:, None, :]).astype(jnp.bfloat16)
    returned = lax.all_to_all(
        feature_grad, "table", split_axis=0, concat_axis=0, tiled=True
    ).reshape(owners * samples, feature_grad.shape[-1])
    window_grad = jnp.dot(counts_t, returned, preferred_element_type=jnp.float32)
    row_select = (jnp.arange(table.shape[1], dtype=jnp.int32)[:, None] == window[None, :]).astype(
        jnp.float32
    )
    row_grad = jnp.dot(row_select, window_grad, precision=lax.Precision.HIGHEST)
    groups = lax.axis_size("expert")
    group_rows = lax.all_to_all(
        row_grad.reshape(groups, row_grad.shape[0] // groups, row_grad.shape[-1]),
        "expert",
        split_axis=0,
        concat_axis=0,
        tiled=True,
    )
    table_grad = jnp.sum(group_rows, axis=0)

    all_rows = lax.all_gather(rows, "expert", axis=0, tiled=True)
    all_grads = lax.all_gather(row_grads, "expert", axis=0, tiled=True)
    shard_pre = jnp.dot(all_rows, weight_in, preferred_element_type=jnp.float32)
    shard_hidden = jax.nn.silu(shard_pre).astype(jnp.bfloat16)
    shard_grad_hidden = lax.dot_general(
        all_grads, weight_out, contract_cols, preferred_element_type=jnp.float32
    )
    shard_grad_pre = (shard_grad_hidden * silu_slope(shard_pre)).astype(jnp.bfloat16)
    grad_out = lax.dot_general(
        shard_hidden, all_grads, contract_rows, preferred_element_type=jnp.float32
    )
    grad_in = lax.dot_general(
        all_rows, shard_grad_pre, contract_rows, preferred_element_type=jnp.float32
    )
    return (predicted[None], table_grad[None], grad_in[None], grad_out[None])


def solution(mesh):
    in_specs = (
        P("table", None, None),
        P("table", None),
        P("table", "expert", None),
        P("table", "expert", None, None),
        P("table", "expert", None),
        P(),
        P(),
        P("expert", "table", None),
        P("table", None, "expert"),
        P("table", "expert", None),
        P(),
        P(),
        P("expert", "table", None),
    )
    out_specs = (
        P("expert", "table", None),
        P("table", "expert", None),
        P("table", None, "expert"),
        P("table", "expert", None),
    )
    return jax.shard_map(local, mesh=mesh, in_specs=in_specs, out_specs=out_specs, check_vma=False)
```

time: 663 us -> 427 us (0.64)
  waiting for transfers between devices: 397 us -> 244 us
  other arithmetic: 58.2 us -> 20.2 us
  blocking collectives: 96 us -> 61.7 us
  local copies, waits for them, and re-layouts: 37.5 us -> 7.22 us
  starting transfers between devices: 26.6 us -> 39.5 us
  matrix products: 31.3 us -> 39.5 us
    reduce_scatter x3 -> x0, waiting for transfers between devices: 113 us -> none  [the longest x2 75.1 us: column_sum(): lax.psum_scatter(term_fn(jnp.int32(0), lax.axis_size('expert') * local_ro...]
    all_to_all x1, waiting for transfers between devices: 122 us -> 45.4 us  [local(): lax.all_to_all(feature_grad, 'table', split_axis=0, concat_axis=0, tiled=...]
    reduce_sum x16 -> x2, other arithmetic: 47.3 us -> 11.9 us  [the longest x1 11.3 us: bag_counts_t(): return jnp.sum(hits, axis=0).astype(jnp.bfloat16)]
    all_to_all x4 -> x3, blocking collectives: 96 us -> 61.7 us  [to_owners(): lax.all_to_all(shaped, 'table', split_axis=0, concat_axis=0, tiled=True)]
    all_gather x2 -> x4, waiting for transfers between devices: 45.6 us -> 64.8 us  [the longest x1 37.6 us: local(): all_rows = lax.all_gather(rows, 'expert', axis=0, tiled=True)]
    eq x32 -> x0, local copies, waits for them, and re-layouts: 13.6 us -> none  [count_block(): block_idx[:, :, None] == positions[None, None, :]]
    all_to_all x0 -> x2, starting transfers between devices: none -> 13 us  [the longest x1 8.8 us: to_owners(): lax.all_to_all(shaped, 'table', split_axis=0, concat_axis=0, tiled=True)]
    all_to_all x0 -> x2, waiting for transfers between devices: none -> 12.3 us  [the longest x1 6.22 us: to_owners(): lax.all_to_all(shaped, 'table', split_axis=0, concat_axis=0, tiled=True)]
  transfers between devices with their start and end apart: 7 -> 8, of which waited for: 7 -> 6; matrix products, arithmetic and copies ran while one was open for 1% -> 6% of each run, Pallas kernels for 0% -> 0%
where the time goes in v1:
time: 427 us; the launch traced here: 426 us
  waiting for transfers between devices  244 us (57%)
  blocking collectives  61.7 us (14%)
  matrix products  39.5 us (9%)
  starting transfers between devices  39.5 us (9%)
  other arithmetic  20.2 us (5%)
  between operations  14.1 us (3%)
  local copies, waits for them, and re-layouts  7.22 us (2%)
    all_to_all x1, waiting for transfers between devices, local(): lax.all_to_all(pooled.reshape(owners, samples, pooled.shape[-1]), 'table'...  119 us
    all_to_all x3, blocking collectives, to_owners(): lax.all_to_all(shaped, 'table', split_axis=0, concat_axis=0, tiled=True)  61.7 us
    all_to_all x1, waiting for transfers between devices, local(): lax.all_to_all(feature_grad, 'table', split_axis=0, concat_axis=0, tiled=...  45.4 us
    all_gather x1, waiting for transfers between devices, local(): all_rows = lax.all_gather(rows, 'expert', axis=0, tiled=True)  37.6 us
    all_gather x1, waiting for transfers between devices, local(): all_grads = lax.all_gather(row_grads, 'expert', axis=0, tiled=True)  27.1 us
    all_to_all x1, starting transfers between devices, local(): lax.all_to_all(pooled.reshape(owners, samples, pooled.shape[-1]), 'table'...  16.6 us
    reduce_sum x1, other arithmetic, bag_counts_t(): return jnp.sum(hits, axis=0).astype(jnp.bfloat16)  11.3 us
    all_to_all x1, starting transfers between devices, local(): lax.all_to_all(feature_grad, 'table', split_axis=0, concat_axis=0, tiled=...  9.71 us
  transfers between devices with their start and end apart: 8, of which 6 were waited for; matrix products, arithmetic and copies ran while one was open for 6% of the time, Pallas kernels for 0%

profile of v1, /device:TPU:40, one launch (start us, length us, event | category | flops | bytes accessed | tf_op | source)
XLA Modules:
  0.0 425.9 jit_solution(18200819362483395928)
XLA Ops:
  7.2 1.0 bitcast_select_fusion
  8.3 11.3 %convert_reduce_fusion = bf16[256,8192]{1,0:T(8,128)(2,1)} fusion(s32[8,8192]{1,0:T(8,128)S(1)} %bitcast_select_fusion), kind=kLoop, calls=%fused_computation.2 | loop fusion | flops 48234496 | bytes 4456448 | tf_op jit(solution)/shard_map/reduce_sum | solution.py:19
  19.6 1.9 gather_fusion.1
  21.5 1.2 gather_fusion
  22.7 5.6 %convolution_convert_fusion = bf16[8192,256]{1,0:T(8,128)(2,1)} fusion(bf16[256,8192]{1,0:T(8,128)(2,1)} %convert_reduce_fusion, f32[256]{0:T(256)S(1)} %get-tuple-element.16, bf16[256,256]{1,0:T(8,128)(2,1)S(1)} %gather_fusion, pred[256]{0:T(512)(128)(4,1)S(1)} %get-tuple-element.17), kind=kOutput, calls=%fused_computation.4 | convolution fusion | flops 1076166656 | bytes 8520960 | tf_op jit(solution)/shard_map/dot_general | solution.py:68
  28.3 16.6 %all-to-all-start = ((bf16[64,128,256]{2,1,0:T(8,128)(2,1)}), bf16[64,128,256]{2,1,0:T(8,128)(2,1)}, u32[]{:S(2)}, u32[]{:S(2)}) async-start(bf16[64,128,256]{2,1,0:T(8,128)(2,1)} %bitcast.100), calls=%async_computation | async-start | bytes 8388608 | tf_op jit(solution)/shard_map/all_to_all | solution.py:71
  45.7 0.7 all-gather.13.cloned.1.call-update
  46.8 118.8 %all-to-all-done = bf16[64,128,256]{2,1,0:T(8,128)(2,1)} async-done(((bf16[64,128,256]{2,1,0:T(8,128)(2,1)}), bf16[64,128,256]{2,1,0:T(8,128)(2,1)}, u32[]{:S(2)}, u32[]{:S(2)}) %all-to-all-start) | async-done | bytes 4194336 | tf_op jit(solution)/shard_map/all_to_all | solution.py:71
  165.6 3.1 multiply_reduce_fusion
  169.1 28.4 %all_to_all.35 = bf16[64,4,256]{2,1,0:T(4,128)(2,1)S(1)} all-to-all(bf16[64,4,256]{2,1,0:T(4,128)(2,1)S(1)} %reshape.180), channel_id=1, replica_groups=mesh['table'=64,'expert'=8] {'table'}, dimensions={0} | all-to-all | bytes 262144 | tf_op jit(solution)/shard_map/all_to_all | solution.py:24
  197.6 4.9 %multiply_convert_fusion.3 = (bf16[256,4096]{1,0:T(8,128)(2,1)S(1)}, f32[256,4096]{1,0:T(8,128)}) fusion(bf16[256,256]{1,0:T(8,128)(2,1)S(1)} %reshape.181, bf16[1,256,4096]{2,1,0:T(8,128)(2,1)} %all-gather.11.cloned.1.call-done), kind=kOutput, calls=%fused_computation.12 | convolution fusion | flops 542113792 | bytes 8519680 | tf_op jit(solution)/shard_map/dot_general | solution.py:92
  202.6 2.3 fusion.24
  205.0 16.7 %all_to_all.36 = bf16[64,4,256]{2,1,0:T(4,128)(2,1)S(1)} all-to-all(bf16[64,4,256]{2,1,0:T(4,128)(2,1)S(1)} %reshape.184), channel_id=1, replica_groups=mesh['table'=64,'expert'=8] {'table'}, dimensions={0} | all-to-all | bytes 262144 | tf_op jit(solution)/shard_map/all_to_all | solution.py:24
  222.7 0.7 reshape.186
  223.4 8.8 %all-to-all-start.3 = ((bf16[64,4,256]{2,1,0:T(4,128)(2,1)}), bf16[64,4,256]{2,1,0:T(4,128)(2,1)S(1)}, u32[]{:S(2)}, u32[]{:S(2)}) async-start(bf16[64,4,256]{2,1,0:T(4,128)(2,1)} %reshape.186), calls=%async_computation.3 | async-start | bytes 262144 | tf_op jit(solution)/shard_map/all_to_all | solution.py:24
  232.3 2.5 copy.26
  234.8 6.2 %all-to-all-done.3 = bf16[64,4,256]{2,1,0:T(4,128)(2,1)S(1)} async-done(((bf16[64,4,256]{2,1,0:T(4,128)(2,1)}), bf16[64,4,256]{2,1,0:T(4,128)(2,1)S(1)}, u32[]{:S(2)}, u32[]{:S(2)}) %all-to-all-start.3) | async-done | bytes 131104 | tf_op jit(solution)/shard_map/all_to_all | solution.py:24
  241.1 4.7 %fusion = bf16[256,4096]{1,0:T(8,128)(2,1)S(1)} fusion(bf16[256,256]{1,0:T(8,128)(2,1)S(1)} %reshape.187, f32[256,4096]{1,0:T(8,128)} %get-tuple-element.24, bf16[1,4096,256]{2,1,0:T(8,128)(2,1)} %all-gather.13.cloned.1.call-done), kind=kOutput, calls=%fused_computation.8 | convolution fusion | flops 546308096 | bytes 8519680 | tf_op jit(solution)/shard_map/dot_general | solution.py:115
  245.8 0.7 fusion.21
  246.6 16.6 %all_to_all.37 = bf16[64,4,256]{2,1,0:T(4,128)(2,1)S(1)} all-to-all(bf16[64,4,256]{2,1,0:T(4,128)(2,1)S(1)} %reshape.190), channel_id=1, replica_groups=mesh['table'=64,'expert'=8] {'table'}, dimensions={0} | all-to-all | bytes 262144 | tf_op jit(solution)/shard_map/all_to_all | solution.py:24
  263.6 3.4 multiply_convert_fusion
  267.0 9.7 %all-to-all-start.5 = ((bf16[64,128,256]{2,1,0:T(8,128)(2,1)}), bf16[64,128,256]{2,1,0:T(8,128)(2,1)}, u32[]{:S(2)}, u32[]{:S(2)}) async-start(bf16[64,128,256]{2,1,0:T(8,128)(2,1)} %multiply_convert_fusion), calls=%async_computation.5 | async-start | bytes 8388608 | tf_op jit(solution)/shard_map/all_to_all | solution.py:130
  278.6 37.6 %all-gather.7.cloned.1.call-done = bf16[2048,256]{1,0:T(8,128)(2,1)} async-done(((bf16[256,256]{1,0:T(8,128)(2,1)}), bf16[2048,256]{1,0:T(8,128)(2,1)}) %all-gather.7.cloned.1.call-update) | async-done | bytes 1048592 | tf_op jit(solution)/shard_map/all_gather | solution.py:148
  316.2 4.0 fusion.34
  320.2 27.1 %all-gather.9.cloned.1.call-done = bf16[2048,256]{1,0:T(8,128)(2,1)} async-done(((bf16[256,256]{1,0:T(8,128)(2,1)}), bf16[2048,256]{1,0:T(8,128)(2,1)}) %all-gather.9.cloned.1.call-update) | async-done | bytes 1048592 | tf_op jit(solution)/shard_map/all_gather | solution.py:149
  347.3 5.4 %fusion.27 = f32[1,256,512]{2,1,0:T(8,128)} fusion(bf16[2048,256]{1,0:T(8,128)(2,1)S(1)} %copy-done.3, f32[2048,512]{1,0:T(8,128)} %fusion.34, bf16[2048,256]{1,0:T(8,128)(2,1)} %all-gather.9.cloned.1.call-done, bf16[1,512,256]{2,1,0:T(8,128)(2,1)S(1)} %copy-done.10), kind=kOutput, calls=%fused_computation.32 | convolution fusion | flops 1083179008 | bytes 7077888 | tf_op jit(solution)/shard_map/dot_general | solution.py:159
  352.7 45.4 %all-to-all-done.5 = bf16[64,128,256]{2,1,0:T(8,128)(2,1)} async-done(((bf16[64,128,256]{2,1,0:T(8,128)(2,1)}), bf16[64,128,256]{2,1,0:T(8,128)(2,1)}, u32[]{:S(2)}, u32[]{:S(2)}) %all-to-all-start.5) | async-done | bytes 4194336 | tf_op jit(solution)/shard_map/all_to_all | solution.py:130
  398.2 4.8 %fusion.61 = f32[256,256]{1,0:T(8,128)S(1)} fusion(bf16[256,8192]{1,0:T(8,128)(2,1)} %convert_reduce_fusion, bf16[8192,256]{1,0:T(8,128)(2,1)} %bitcast.23), kind=kOutput, calls=%fused_computation.97 | convolution fusion | flops 1073741824 | bytes 8650752 | tf_op jit(solution)/shard_map/dot_general | solution.py:133
  403.0 1.2 fusion.33
  404.2 4.2 all-to-all-start.6
  408.4 4.3 %fusion.28 = f32[1,512,256]{2,1,0:T(8,128)} fusion(bf16[2048,256]{1,0:T(8,128)(2,1)S(1)} %copy-done.15, f32[2048,512]{1,0:T(8,128)} %fusion.34), kind=kOutput, calls=%fused_computation.33 | convolution fusion | flops 542113792 | bytes 5767168 | tf_op jit(solution)/shard_map/dot_general | solution.py:156
  412.7 6.0 %all-to-all-done.6 = f32[8,64,256]{2,1,0:T(8,128)S(1)} async-done(((f32[8,64,256]{2,1,0:T(8,128)}), f32[8,64,256]{2,1,0:T(8,128)S(1)}, u32[]{:S(2)}, u32[]{:S(2)}) %all-to-all-start.6) | async-done | bytes 524320 | tf_op jit(solution)/shard_map/all_to_all | solution.py:139
  (70 shorter events, 5.9 us)
Async XLA Ops:
  7.2 214.5 %copy-start = (bf16[3,256,256]{2,1,0:T(8,128)(2,1)S(1)}, bf16[3,256,256]{2,1,0:T(8,128)(2,1)}, u32[]{:S(2)}) copy-start(bf16[3,256,256]{2,1,0:T(8,128)(2,1)} %param.23) | copy-start | bytes 1179652
  7.2 12.4 %copy-start.11 = (s32[1,1,256]{2,1,0:T(1,128)S(1)}, s32[1,1,256]{2,1,0:T(1,128)}, u32[]{:S(2)}) copy-start(s32[1,1,256]{2,1,0:T(1,128)} %param.15) | copy-start | bytes 3076
  7.2 12.4 %copy-start.1 = (f32[1,512]{1,0:T(1,128)S(1)}, f32[1,512]{1,0:T(1,128)}, u32[]{:S(2)}) copy-start(f32[1,512]{1,0:T(1,128)} %param.14) | copy-start | bytes 6148
  7.2 14.3 %copy-start.2 = (bf16[1,512,256]{2,1,0:T(8,128)(2,1)S(1)}, bf16[1,512,256]{2,1,0:T(8,128)(2,1)}, u32[]{:S(2)}) copy-start(bf16[1,512,256]{2,1,0:T(8,128)(2,1)} %param.13) | copy-start | bytes 786436
  28.2 18.1 %copy-start.13 = (s32[1,128,1]{1,2,0:T(1,128)S(1)}, s32[1,128,1]{1,2,0:T(1,128)}, u32[]{:S(2)}) copy-start(s32[1,128,1]{1,2,0:T(1,128)} %param.20) | copy-start | bytes 1540
  28.2 137.4 %copy-start.9 = (f32[64,256]{1,0:T(8,128)S(1)}, f32[64,256]{1,0:T(8,128)}, u32[]{:S(2)}) copy-start(f32[64,256]{1,0:T(8,128)} %param.18) | copy-start | bytes 196612
  28.3 137.3 %all-to-all-start = ((bf16[64,128,256]{2,1,0:T(8,128)(2,1)}), bf16[64,128,256]{2,1,0:T(8,128)(2,1)}, u32[]{:S(2)}, u32[]{:S(2)}) async-start(bf16[64,128,256]{2,1,0:T(8,128)(2,1)} %bitcast.100), calls=%async_computation | async-start | bytes 8388608 | tf_op jit(solution)/shard_map/all_to_all | solution.py:71
  44.9 124.0 %copy-start.12 = (f32[256]{0:T(256)S(1)}, f32[256]{0:T(256)}, u32[]{:S(2)}) copy-start(f32[256]{0:T(256)} %param.19) | copy-start | bytes 3076
  44.9 152.8 %all-gather.11.cloned.1.call-start = ((), (), s32[]{:S(2)}) async-start(), calls=%async_computation.9 | async-start | bytes 2359296 | tf_op jit(solution)/shard_map/all_gather | solution.py:59
  45.6 157.0 %all-gather.13.cloned.1.call-start = ((), (), s32[]{:S(2)}) async-start(), calls=%async_computation.10 | async-start | bytes 2359296 | tf_op jit(solution)/shard_map/all_gather | solution.py:60
  197.6 5.0 %copy-start.7 = (bf16[256,256]{1,0:T(8,128)(2,1)}, bf16[256,256]{1,0:T(8,128)(2,1)S(1)}, u32[]{:S(2)}) copy-start(bf16[256,256]{1,0:T(8,128)(2,1)S(1)} %reshape.181) | copy-start | bytes 393220
  202.6 19.1 %copy-start.16 = (f32[3,256]{1,0:T(4,128)S(1)}, f32[3,256]{1,0:T(4,128)}, u32[]{:S(2)}) copy-start(f32[3,256]{1,0:T(4,128)} %param.24) | copy-start | bytes 9220
  202.6 19.6 %copy-start.14 = (f32[1,128,3]{1,0,2:T(1,128)S(1)}, f32[1,128,3]{1,0,2:T(1,128)}, u32[]{:S(2)}) copy-start(f32[1,128,3]{1,0,2:T(1,128)} %param.25) | copy-start | bytes 4612
  204.9 27.3 %copy-start.4 = (bf16[1,256,4096]{2,1,0:T(8,128)(2,1)S(1)}, bf16[1,256,4096]{2,1,0:T(8,128)(2,1)}, u32[]{:S(2)}) copy-start(bf16[1,256,4096]{2,1,0:T(8,128)(2,1)} %all-gather.11.cloned.1.call-done) | copy-start | bytes 6291460
  223.4 17.6 %all-to-all-start.3 = ((bf16[64,4,256]{2,1,0:T(4,128)(2,1)}), bf16[64,4,256]{2,1,0:T(4,128)(2,1)S(1)}, u32[]{:S(2)}, u32[]{:S(2)}) async-start(bf16[64,4,256]{2,1,0:T(4,128)(2,1)} %reshape.186), calls=%async_computation.3 | async-start | bytes 262144 | tf_op jit(solution)/shard_map/all_to_all | solution.py:24
  241.0 4.7 %copy-start.8 = (bf16[256,256]{1,0:T(8,128)(2,1)}, bf16[256,256]{1,0:T(8,128)(2,1)S(1)}, u32[]{:S(2)}) copy-start(bf16[256,256]{1,0:T(8,128)(2,1)S(1)} %reshape.187) | copy-start | bytes 393220
  241.1 4.7 %copy-start.5 = (bf16[4096,256]{1,0:T(8,128)(2,1)S(1)}, bf16[4096,256]{1,0:T(8,128)(2,1)}, u32[]{:S(2)}) copy-start(bf16[4096,256]{1,0:T(8,128)(2,1)} %copy.26) | copy-start | bytes 6291460
  267.0 49.2 %copy-start.6 = (bf16[1,256,512]{2,1,0:T(8,128)(2,1)S(1)}, bf16[1,256,512]{2,1,0:T(8,128)(2,1)}, u32[]{:S(2)}) copy-start(bf16[1,256,512]{2,1,0:T(8,128)(2,1)} %param.21) | copy-start | bytes 786436
  267.0 131.2 %all-to-all-start.5 = ((bf16[64,128,256]{2,1,0:T(8,128)(2,1)}), bf16[64,128,256]{2,1,0:T(8,128)(2,1)}, u32[]{:S(2)}, u32[]{:S(2)}) async-start(bf16[64,128,256]{2,1,0:T(8,128)(2,1)} %multiply_convert_fusion), calls=%async_computation.5 | async-start | bytes 8388608 | tf_op jit(solution)/shard_map/all_to_all | solution.py:130
  276.7 39.5 %all-gather.7.cloned.1.call-start = ((), (), s32[]{:S(2)}) async-start(), calls=%async_computation.7 | async-start | bytes 1179648 | tf_op jit(solution)/shard_map/all_gather | solution.py:148
  277.5 69.9 %all-gather.9.cloned.1.call-start = ((), (), s32[]{:S(2)}) async-start(), calls=%async_computation.8 | async-start | bytes 1179648 | tf_op jit(solution)/shard_map/all_gather | solution.py:149
  278.6 68.7 %copy-start.10 = (bf16[1,512,256]{2,1,0:T(8,128)(2,1)S(1)}, bf16[1,512,256]{2,1,0:T(8,128)(2,1)}, u32[]{:S(2)}) copy-start(bf16[1,512,256]{2,1,0:T(8,128)(2,1)} %param.22) | copy-start | bytes 786436
  316.2 31.1 %copy-start.3 = (bf16[2048,256]{1,0:T(8,128)(2,1)S(1)}, bf16[2048,256]{1,0:T(8,128)(2,1)}, u32[]{:S(2)}) copy-start(bf16[2048,256]{1,0:T(8,128)(2,1)} %all-gather.7.cloned.1.call-done) | copy-start | bytes 3145732
  398.2 10.2 %copy-start.15 = (bf16[2048,256]{1,0:T(8,128)(2,1)S(1)}, bf16[2048,256]{1,0:T(8,128)(2,1)}, u32[]{:S(2)}) copy-start(bf16[2048,256]{1,0:T(8,128)(2,1)} %all-gather.9.cloned.1.call-done) | copy-start | bytes 3145732
  404.2 14.5 %all-to-all-start.6 = ((f32[8,64,256]{2,1,0:T(8,128)}), f32[8,64,256]{2,1,0:T(8,128)S(1)}, u32[]{:S(2)}, u32[]{:S(2)}) async-start(f32[8,64,256]{2,1,0:T(8,128)} %bitcast.24), calls=%async_computation.6 | async-start | bytes 1048576 | tf_op jit(solution)/shard_map/all_to_all | solution.py:139
Sparse Core Ops, SparseCore 0:
  47.8 31.2 all-gather.10
  81.2 30.9 all-gather.12
  280.2 35.9 all-gather.6
  318.8 28.4 all-gather.8

commit v2 on v1

--- a/solution.py
+++ b/solution.py
@@ -2,6 +2,7 @@
 import jax.numpy as jnp
 from jax import lax
 from jax.sharding import PartitionSpec as P
+
 
 code_range = 127.0
 
@@ -33,7 +34,7 @@
     return jnp.sum(partials.astype(jnp.bfloat16).astype(jnp.float32), axis=0).astype(jnp.bfloat16)
 
 
-def local(
+def step(
     table,
     row_scale,
     windows,
@@ -89,9 +90,11 @@
     )
     outgoing = jnp.dot(placing, normed, preferred_element_type=jnp.float32).astype(jnp.bfloat16)
     rows = to_owners(outgoing, owners)
+    all_rows = lax.all_gather(rows, "expert", axis=0, tiled=True)
     pre_act = jnp.dot(rows, full_in, preferred_element_type=jnp.float32)
     hidden = jax.nn.silu(pre_act).astype(jnp.bfloat16)
-    expert_out = to_owners(shard_partials(hidden, full_out, shards), owners)
+    expert_partial = shard_partials(hidden, full_out, shards)
+    expert_out = to_owners(expert_partial, owners)
     mixture = lax.dot_general(
         placing, expert_out, contract_rows, preferred_element_type=jnp.float32
     )
@@ -112,11 +115,13 @@
         jnp.bfloat16
     )
     row_grads = to_owners(back_rows, owners)
+    all_grads = lax.all_gather(row_grads, "expert", axis=0, tiled=True)
     grad_hidden = lax.dot_general(
         row_grads, full_out, contract_cols, preferred_element_type=jnp.float32
     )
     grad_pre = (grad_hidden * silu_slope(pre_act)).astype(jnp.bfloat16)
-    input_grad = to_owners(shard_partials(grad_pre, full_in.T, shards), owners)
+    input_partial = shard_partials(grad_pre, full_in.T, shards)
+    input_grad = to_owners(input_partial, owners)
     mixture_grad = lax.dot_general(
         placing, input_grad, contract_rows, preferred_element_type=jnp.float32
     )
@@ -145,8 +150,6 @@
     )
     table_grad = jnp.sum(group_rows, axis=0)
 
-    all_rows = lax.all_gather(rows, "expert", axis=0, tiled=True)
-    all_grads = lax.all_gather(row_grads, "expert", axis=0, tiled=True)
     shard_pre = jnp.dot(all_rows, weight_in, preferred_element_type=jnp.float32)
     shard_hidden = jax.nn.silu(shard_pre).astype(jnp.bfloat16)
     shard_grad_hidden = lax.dot_general(
@@ -184,4 +187,4 @@
         P("table", None, "expert"),
         P("table", "expert", None),
     )
-    return jax.shard_map(local, mesh=mesh, in_specs=in_specs, out_specs=out_specs, check_vma=False)
+    return jax.shard_map(step, mesh=mesh, in_specs=in_specs, out_specs=out_specs, check_vma=False)

time: 427 us -> 427 us (level)
  no operation moved by 1% of the time
where the time goes in v2:
time: 427 us; the launch traced here: 426 us
  waiting for transfers between devices  244 us (57%)
  blocking collectives  61.7 us (14%)
  matrix products  39.5 us (9%)
  starting transfers between devices  39.5 us (9%)
  other arithmetic  20.2 us (5%)
  between operations  14.1 us (3%)
  local copies, waits for them, and re-layouts  7.22 us (2%)
    all_to_all x1, waiting for transfers between devices, step(): lax.all_to_all(pooled.reshape(owners, samples, pooled.shape[-1]), 'table'...  119 us
    all_to_all x3, blocking collectives, to_owners(): lax.all_to_all(shaped, 'table', split_axis=0, concat_axis=0, tiled=True)  61.7 us
    all_to_all x1, waiting for transfers between devices, step(): lax.all_to_all(feature_grad, 'table', split_axis=0, concat_axis=0, tiled=...  45.4 us
    all_gather x1, waiting for transfers between devices, step(): all_rows = lax.all_gather(rows, 'expert', axis=0, tiled=True)  37.6 us
    all_gather x1, waiting for transfers between devices, step(): all_grads = lax.all_gather(row_grads, 'expert', axis=0, tiled=True)  27.1 us
    all_to_all x1, starting transfers between devices, step(): lax.all_to_all(pooled.reshape(owners, samples, pooled.shape[-1]), 'table'...  16.6 us
    reduce_sum x1, other arithmetic, bag_counts_t(): return jnp.sum(hits, axis=0).astype(jnp.bfloat16)  11.3 us
    all_to_all x1, starting transfers between devices, step(): lax.all_to_all(feature_grad, 'table', split_axis=0, concat_axis=0, tiled=...  9.71 us
  transfers between devices with their start and end apart: 8, of which 6 were waited for; matrix products, arithmetic and copies ran while one was open for 6% of the time, Pallas kernels for 0%

profile of v2, /device:TPU:40, one launch (start us, length us, event | category | flops | bytes accessed | tf_op | source)
XLA Modules:
  0.0 425.9 jit_solution(18200819362483395928)
XLA Ops:
  7.2 1.0 bitcast_select_fusion
  8.3 11.3 %convert_reduce_fusion = bf16[256,8192]{1,0:T(8,128)(2,1)} fusion(s32[8,8192]{1,0:T(8,128)S(1)} %bitcast_select_fusion), kind=kLoop, calls=%fused_computation.2 | loop fusion | flops 48234496 | bytes 4456448 | tf_op jit(solution)/shard_map/reduce_sum | solution.py:20
  19.6 1.9 gather_fusion.1
  21.5 1.2 gather_fusion
  22.7 5.6 %convolution_convert_fusion = bf16[8192,256]{1,0:T(8,128)(2,1)} fusion(bf16[256,8192]{1,0:T(8,128)(2,1)} %convert_reduce_fusion, f32[256]{0:T(256)S(1)} %get-tuple-element.16, bf16[256,256]{1,0:T(8,128)(2,1)S(1)} %gather_fusion, pred[256]{0:T(512)(128)(4,1)S(1)} %get-tuple-element.17), kind=kOutput, calls=%fused_computation.4 | convolution fusion | flops 1076166656 | bytes 8520960 | tf_op jit(solution)/shard_map/dot_general | solution.py:69
  28.3 16.6 %all-to-all-start = ((bf16[64,128,256]{2,1,0:T(8,128)(2,1)}), bf16[64,128,256]{2,1,0:T(8,128)(2,1)}, u32[]{:S(2)}, u32[]{:S(2)}) async-start(bf16[64,128,256]{2,1,0:T(8,128)(2,1)} %bitcast.100), calls=%async_computation | async-start | bytes 8388608 | tf_op jit(solution)/shard_map/all_to_all | solution.py:72
  45.7 0.7 all-gather.13.cloned.1.call-update
  46.8 118.8 %all-to-all-done = bf16[64,128,256]{2,1,0:T(8,128)(2,1)} async-done(((bf16[64,128,256]{2,1,0:T(8,128)(2,1)}), bf16[64,128,256]{2,1,0:T(8,128)(2,1)}, u32[]{:S(2)}, u32[]{:S(2)}) %all-to-all-start) | async-done | bytes 4194336 | tf_op jit(solution)/shard_map/all_to_all | solution.py:72
  165.6 3.1 multiply_reduce_fusion
  169.1 28.4 %all_to_all.35 = bf16[64,4,256]{2,1,0:T(4,128)(2,1)S(1)} all-to-all(bf16[64,4,256]{2,1,0:T(4,128)(2,1)S(1)} %reshape.180), channel_id=1, replica_groups=mesh['table'=64,'expert'=8] {'table'}, dimensions={0} | all-to-all | bytes 262144 | tf_op jit(solution)/shard_map/all_to_all | solution.py:25
  197.6 4.9 %multiply_convert_fusion.3 = (bf16[256,4096]{1,0:T(8,128)(2,1)S(1)}, f32[256,4096]{1,0:T(8,128)}) fusion(bf16[256,256]{1,0:T(8,128)(2,1)S(1)} %reshape.181, bf16[1,256,4096]{2,1,0:T(8,128)(2,1)} %all-gather.11.cloned.1.call-done), kind=kOutput, calls=%fused_computation.12 | convolution fusion | flops 542113792 | bytes 8519680 | tf_op jit(solution)/shard_map/dot_general | solution.py:94
  202.6 2.3 fusion.24
  205.0 16.7 %all_to_all.36 = bf16[64,4,256]{2,1,0:T(4,128)(2,1)S(1)} all-to-all(bf16[64,4,256]{2,1,0:T(4,128)(2,1)S(1)} %reshape.184), channel_id=1, replica_groups=mesh['table'=64,'expert'=8] {'table'}, dimensions={0} | all-to-all | bytes 262144 | tf_op jit(solution)/shard_map/all_to_all | solution.py:25
  222.7 0.7 reshape.186
  223.4 8.8 %all-to-all-start.3 = ((bf16[64,4,256]{2,1,0:T(4,128)(2,1)}), bf16[64,4,256]{2,1,0:T(4,128)(2,1)S(1)}, u32[]{:S(2)}, u32[]{:S(2)}) async-start(bf16[64,4,256]{2,1,0:T(4,128)(2,1)} %reshape.186), calls=%async_computation.3 | async-start | bytes 262144 | tf_op jit(solution)/shard_map/all_to_all | solution.py:25
  232.3 2.5 copy.26
  234.8 6.2 %all-to-all-done.3 = bf16[64,4,256]{2,1,0:T(4,128)(2,1)S(1)} async-done(((bf16[64,4,256]{2,1,0:T(4,128)(2,1)}), bf16[64,4,256]{2,1,0:T(4,128)(2,1)S(1)}, u32[]{:S(2)}, u32[]{:S(2)}) %all-to-all-start.3) | async-done | bytes 131104 | tf_op jit(solution)/shard_map/all_to_all | solution.py:25
  241.1 4.7 %fusion = bf16[256,4096]{1,0:T(8,128)(2,1)S(1)} fusion(bf16[256,256]{1,0:T(8,128)(2,1)S(1)} %reshape.187, f32[256,4096]{1,0:T(8,128)} %get-tuple-element.24, bf16[1,4096,256]{2,1,0:T(8,128)(2,1)} %all-gather.13.cloned.1.call-done), kind=kOutput, calls=%fused_computation.8 | convolution fusion | flops 546308096 | bytes 8519680 | tf_op jit(solution)/shard_map/dot_general | solution.py:119
  245.8 0.7 fusion.21
  246.6 16.6 %all_to_all.37 = bf16[64,4,256]{2,1,0:T(4,128)(2,1)S(1)} all-to-all(bf16[64,4,256]{2,1,0:T(4,128)(2,1)S(1)} %reshape.190), channel_id=1, replica_groups=mesh['table'=64,'expert'=8] {'table'}, dimensions={0} | all-to-all | bytes 262144 | tf_op jit(solution)/shard_map/all_to_all | solution.py:25
  263.6 3.4 multiply_convert_fusion
  267.0 9.7 %all-to-all-start.5 = ((bf16[64,128,256]{2,1,0:T(8,128)(2,1)}), bf16[64,128,256]{2,1,0:T(8,128)(2,1)}, u32[]{:S(2)}, u32[]{:S(2)}) async-start(bf16[64,128,256]{2,1,0:T(8,128)(2,1)} %multiply_convert_fusion), calls=%async_computation.5 | async-start | bytes 8388608 | tf_op jit(solution)/shard_map/all_to_all | solution.py:135
  278.6 37.6 %all-gather.7.cloned.1.call-done = bf16[2048,256]{1,0:T(8,128)(2,1)} async-done(((bf16[256,256]{1,0:T(8,128)(2,1)}), bf16[2048,256]{1,0:T(8,128)(2,1)}) %all-gather.7.cloned.1.call-update) | async-done | bytes 1048592 | tf_op jit(solution)/shard_map/all_gather | solution.py:93
  316.2 4.0 fusion.34
  320.2 27.1 %all-gather.9.cloned.1.call-done = bf16[2048,256]{1,0:T(8,128)(2,1)} async-done(((bf16[256,256]{1,0:T(8,128)(2,1)}), bf16[2048,256]{1,0:T(8,128)(2,1)}) %all-gather.9.cloned.1.call-update) | async-done | bytes 1048592 | tf_op jit(solution)/shard_map/all_gather | solution.py:118
  347.3 5.4 %fusion.27 = f32[1,256,512]{2,1,0:T(8,128)} fusion(bf16[2048,256]{1,0:T(8,128)(2,1)S(1)} %copy-done.3, f32[2048,512]{1,0:T(8,128)} %fusion.34, bf16[2048,256]{1,0:T(8,128)(2,1)} %all-gather.9.cloned.1.call-done, bf16[1,512,256]{2,1,0:T(8,128)(2,1)S(1)} %copy-done.10), kind=kOutput, calls=%fused_computation.32 | convolution fusion | flops 1083179008 | bytes 7077888 | tf_op jit(solution)/shard_map/dot_general | solution.py:162
  352.7 45.4 %all-to-all-done.5 = bf16[64,128,256]{2,1,0:T(8,128)(2,1)} async-done(((bf16[64,128,256]{2,1,0:T(8,128)(2,1)}), bf16[64,128,256]{2,1,0:T(8,128)(2,1)}, u32[]{:S(2)}, u32[]{:S(2)}) %all-to-all-start.5) | async-done | bytes 4194336 | tf_op jit(solution)/shard_map/all_to_all | solution.py:135
  398.2 4.8 %fusion.61 = f32[256,256]{1,0:T(8,128)S(1)} fusion(bf16[256,8192]{1,0:T(8,128)(2,1)} %convert_reduce_fusion, bf16[8192,256]{1,0:T(8,128)(2,1)} %bitcast.23), kind=kOutput, calls=%fused_computation.97 | convolution fusion | flops 1073741824 | bytes 8650752 | tf_op jit(solution)/shard_map/dot_general | solution.py:138
  403.0 1.2 fusion.33
  404.2 4.2 all-to-all-start.6
  408.4 4.3 %fusion.28 = f32[1,512,256]{2,1,0:T(8,128)} fusion(bf16[2048,256]{1,0:T(8,128)(2,1)S(1)} %copy-done.15, f32[2048,512]{1,0:T(8,128)} %fusion.34), kind=kOutput, calls=%fused_computation.33 | convolution fusion | flops 542113792 | bytes 5767168 | tf_op jit(solution)/shard_map/dot_general | solution.py:159
  412.7 6.0 %all-to-all-done.6 = f32[8,64,256]{2,1,0:T(8,128)S(1)} async-done(((f32[8,64,256]{2,1,0:T(8,128)}), f32[8,64,256]{2,1,0:T(8,128)S(1)}, u32[]{:S(2)}, u32[]{:S(2)}) %all-to-all-start.6) | async-done | bytes 524320 | tf_op jit(solution)/shard_map/all_to_all | solution.py:144
  (70 shorter events, 5.9 us)
Async XLA Ops:
  7.2 214.5 %copy-start = (bf16[3,256,256]{2,1,0:T(8,128)(2,1)S(1)}, bf16[3,256,256]{2,1,0:T(8,128)(2,1)}, u32[]{:S(2)}) copy-start(bf16[3,256,256]{2,1,0:T(8,128)(2,1)} %param.23) | copy-start | bytes 1179652
  7.2 12.4 %copy-start.11 = (s32[1,1,256]{2,1,0:T(1,128)S(1)}, s32[1,1,256]{2,1,0:T(1,128)}, u32[]{:S(2)}) copy-start(s32[1,1,256]{2,1,0:T(1,128)} %param.15) | copy-start | bytes 3076
  7.2 12.4 %copy-start.1 = (f32[1,512]{1,0:T(1,128)S(1)}, f32[1,512]{1,0:T(1,128)}, u32[]{:S(2)}) copy-start(f32[1,512]{1,0:T(1,128)} %param.14) | copy-start | bytes 6148
  7.2 14.3 %copy-start.2 = (bf16[1,512,256]{2,1,0:T(8,128)(2,1)S(1)}, bf16[1,512,256]{2,1,0:T(8,128)(2,1)}, u32[]{:S(2)}) copy-start(bf16[1,512,256]{2,1,0:T(8,128)(2,1)} %param.13) | copy-start | bytes 786436
  28.2 18.1 %copy-start.13 = (s32[1,128,1]{1,2,0:T(1,128)S(1)}, s32[1,128,1]{1,2,0:T(1,128)}, u32[]{:S(2)}) copy-start(s32[1,128,1]{1,2,0:T(1,128)} %param.20) | copy-start | bytes 1540
  28.2 137.4 %copy-start.9 = (f32[64,256]{1,0:T(8,128)S(1)}, f32[64,256]{1,0:T(8,128)}, u32[]{:S(2)}) copy-start(f32[64,256]{1,0:T(8,128)} %param.18) | copy-start | bytes 196612
  28.3 137.3 %all-to-all-start = ((bf16[64,128,256]{2,1,0:T(8,128)(2,1)}), bf16[64,128,256]{2,1,0:T(8,128)(2,1)}, u32[]{:S(2)}, u32[]{:S(2)}) async-start(bf16[64,128,256]{2,1,0:T(8,128)(2,1)} %bitcast.100), calls=%async_computation | async-start | bytes 8388608 | tf_op jit(solution)/shard_map/all_to_all | solution.py:72
  44.9 124.0 %copy-start.12 = (f32[256]{0:T(256)S(1)}, f32[256]{0:T(256)}, u32[]{:S(2)}) copy-start(f32[256]{0:T(256)} %param.19) | copy-start | bytes 3076
  44.9 152.8 %all-gather.11.cloned.1.call-start = ((), (), s32[]{:S(2)}) async-start(), calls=%async_computation.9 | async-start | bytes 2359296 | tf_op jit(solution)/shard_map/all_gather | solution.py:60
  45.6 157.0 %all-gather.13.cloned.1.call-start = ((), (), s32[]{:S(2)}) async-start(), calls=%async_computation.10 | async-start | bytes 2359296 | tf_op jit(solution)/shard_map/all_gather | solution.py:61
  197.6 5.0 %copy-start.7 = (bf16[256,256]{1,0:T(8,128)(2,1)}, bf16[256,256]{1,0:T(8,128)(2,1)S(1)}, u32[]{:S(2)}) copy-start(bf16[256,256]{1,0:T(8,128)(2,1)S(1)} %reshape.181) | copy-start | bytes 393220
  202.6 19.1 %copy-start.16 = (f32[3,256]{1,0:T(4,128)S(1)}, f32[3,256]{1,0:T(4,128)}, u32[]{:S(2)}) copy-start(f32[3,256]{1,0:T(4,128)} %param.24) | copy-start | bytes 9220
  202.6 19.6 %copy-start.14 = (f32[1,128,3]{1,0,2:T(1,128)S(1)}, f32[1,128,3]{1,0,2:T(1,128)}, u32[]{:S(2)}) copy-start(f32[1,128,3]{1,0,2:T(1,128)} %param.25) | copy-start | bytes 4612
  204.9 27.3 %copy-start.4 = (bf16[1,256,4096]{2,1,0:T(8,128)(2,1)S(1)}, bf16[1,256,4096]{2,1,0:T(8,128)(2,1)}, u32[]{:S(2)}) copy-start(bf16[1,256,4096]{2,1,0:T(8,128)(2,1)} %all-gather.11.cloned.1.call-done) | copy-start | bytes 6291460
  223.4 17.6 %all-to-all-start.3 = ((bf16[64,4,256]{2,1,0:T(4,128)(2,1)}), bf16[64,4,256]{2,1,0:T(4,128)(2,1)S(1)}, u32[]{:S(2)}, u32[]{:S(2)}) async-start(bf16[64,4,256]{2,1,0:T(4,128)(2,1)} %reshape.186), calls=%async_computation.3 | async-start | bytes 262144 | tf_op jit(solution)/shard_map/all_to_all | solution.py:25
  241.0 4.7 %copy-start.8 = (bf16[256,256]{1,0:T(8,128)(2,1)}, bf16[256,256]{1,0:T(8,128)(2,1)S(1)}, u32[]{:S(2)}) copy-start(bf16[256,256]{1,0:T(8,128)(2,1)S(1)} %reshape.187) | copy-start | bytes 393220
  241.1 4.7 %copy-start.5 = (bf16[4096,256]{1,0:T(8,128)(2,1)S(1)}, bf16[4096,256]{1,0:T(8,128)(2,1)}, u32[]{:S(2)}) copy-start(bf16[4096,256]{1,0:T(8,128)(2,1)} %copy.26) | copy-start | bytes 6291460
  267.0 49.2 %copy-start.6 = (bf16[1,256,512]{2,1,0:T(8,128)(2,1)S(1)}, bf16[1,256,512]{2,1,0:T(8,128)(2,1)}, u32[]{:S(2)}) copy-start(bf16[1,256,512]{2,1,0:T(8,128)(2,1)} %param.21) | copy-start | bytes 786436
  267.0 131.2 %all-to-all-start.5 = ((bf16[64,128,256]{2,1,0:T(8,128)(2,1)}), bf16[64,128,256]{2,1,0:T(8,128)(2,1)}, u32[]{:S(2)}, u32[]{:S(2)}) async-start(bf16[64,128,256]{2,1,0:T(8,128)(2,1)} %multiply_convert_fusion), calls=%async_computation.5 | async-start | bytes 8388608 | tf_op jit(solution)/shard_map/all_to_all | solution.py:135
  276.7 39.5 %all-gather.7.cloned.1.call-start = ((), (), s32[]{:S(2)}) async-start(), calls=%async_computation.7 | async-start | bytes 1179648 | tf_op jit(solution)/shard_map/all_gather | solution.py:93
  277.5 69.9 %all-gather.9.cloned.1.call-start = ((), (), s32[]{:S(2)}) async-start(), calls=%async_computation.8 | async-start | bytes 1179648 | tf_op jit(solution)/shard_map/all_gather | solution.py:118
  278.6 68.7 %copy-start.10 = (bf16[1,512,256]{2,1,0:T(8,128)(2,1)S(1)}, bf16[1,512,256]{2,1,0:T(8,128)(2,1)}, u32[]{:S(2)}) copy-start(bf16[1,512,256]{2,1,0:T(8,128)(2,1)} %param.22) | copy-start | bytes 786436
  316.2 31.1 %copy-start.3 = (bf16[2048,256]{1,0:T(8,128)(2,1)S(1)}, bf16[2048,256]{1,0:T(8,128)(2,1)}, u32[]{:S(2)}) copy-start(bf16[2048,256]{1,0:T(8,128)(2,1)} %all-gather.7.cloned.1.call-done) | copy-start | bytes 3145732
  398.2 10.2 %copy-start.15 = (bf16[2048,256]{1,0:T(8,128)(2,1)S(1)}, bf16[2048,256]{1,0:T(8,128)(2,1)}, u32[]{:S(2)}) copy-start(bf16[2048,256]{1,0:T(8,128)(2,1)} %all-gather.9.cloned.1.call-done) | copy-start | bytes 3145732
  404.2 14.5 %all-to-all-start.6 = ((f32[8,64,256]{2,1,0:T(8,128)}), f32[8,64,256]{2,1,0:T(8,128)S(1)}, u32[]{:S(2)}, u32[]{:S(2)}) async-start(f32[8,64,256]{2,1,0:T(8,128)} %bitcast.24), calls=%async_computation.6 | async-start | bytes 1048576 | tf_op jit(solution)/shard_map/all_to_all | solution.py:144
Sparse Core Ops, SparseCore 0:
  47.8 31.2 all-gather.10
  81.2 30.9 all-gather.12
  280.2 35.9 all-gather.6
  318.8 28.4 all-gather.8

commit v3 on v2

--- a/solution.py
+++ b/solution.py
@@ -86,46 +86,61 @@
     slot_of = jnp.sum(ranks * member, axis=1)
     target_slot = chosen * capacity + slot_of
     placing = (jnp.arange(local_rows, dtype=jnp.int32)[:, None] == target_slot[None, :]).astype(
-        jnp.bfloat16
-    )
-    outgoing = jnp.dot(placing, normed, preferred_element_type=jnp.float32).astype(jnp.bfloat16)
-    rows = to_owners(outgoing, owners)
+        jnp.int32
+    )
+    source = jnp.sum(placing * jnp.arange(1, samples + 1, dtype=jnp.int32)[None, :], axis=1)
+    width = normed.shape[-1]
+    lanes = 128 * (-(-(width + 4) // 128))
+    payload = jnp.concatenate(
+        [
+            normed.astype(jnp.float32),
+            targets[0],
+            jnp.ones((samples, 1), jnp.float32),
+            jnp.zeros((samples, lanes - width - 4), jnp.float32),
+        ],
+        axis=1,
+    )
+    padded = jnp.concatenate([jnp.zeros((1, lanes), jnp.float32), payload], axis=0)
+    arrived = to_owners(jnp.take(padded, source, axis=0), owners)
+    rows = arrived[:, :width].astype(jnp.bfloat16)
+    row_targets = arrived[:, width : width + 3]
+    row_live = arrived[:, width + 3 : width + 4]
     all_rows = lax.all_gather(rows, "expert", axis=0, tiled=True)
     pre_act = jnp.dot(rows, full_in, preferred_element_type=jnp.float32)
     hidden = jax.nn.silu(pre_act).astype(jnp.bfloat16)
-    expert_partial = shard_partials(hidden, full_out, shards)
-    expert_out = to_owners(expert_partial, owners)
-    mixture = lax.dot_general(
-        placing, expert_out, contract_rows, preferred_element_type=jnp.float32
-    )
-    joined = (normed.astype(jnp.float32) + mixture).astype(jnp.bfloat16)
+    mixture = shard_partials(hidden, full_out, shards)
+    joined = (rows.astype(jnp.float32) + mixture.astype(jnp.float32)).astype(jnp.bfloat16)
     tower_pre = jnp.einsum("be,kem->kbm", joined, w_tow1, preferred_element_type=jnp.float32)
     logits = jnp.sum(jax.nn.silu(tower_pre) * w_tow2[:, None, :], axis=-1)
     predicted = jnp.stack(
         [jax.nn.sigmoid(logits[0]), jax.nn.sigmoid(logits[1]), logits[2]], axis=-1
     )
-    logit_grad = predicted - targets[0]
+    logit_grad = (predicted - row_targets) * row_live
     tower_grad = (logit_grad.T[:, :, None] * w_tow2[:, None, :] * silu_slope(tower_pre)).astype(
         jnp.bfloat16
     )
     joined_grad = jnp.einsum(
         "kbm,kem->be", tower_grad, w_tow1, preferred_element_type=jnp.float32
     ).astype(jnp.bfloat16)
-    back_rows = jnp.dot(placing, joined_grad, preferred_element_type=jnp.float32).astype(
-        jnp.bfloat16
-    )
-    row_grads = to_owners(back_rows, owners)
+    row_grads = joined_grad
     all_grads = lax.all_gather(row_grads, "expert", axis=0, tiled=True)
     grad_hidden = lax.dot_general(
         row_grads, full_out, contract_cols, preferred_element_type=jnp.float32
     )
     grad_pre = (grad_hidden * silu_slope(pre_act)).astype(jnp.bfloat16)
-    input_partial = shard_partials(grad_pre, full_in.T, shards)
-    input_grad = to_owners(input_partial, owners)
-    mixture_grad = lax.dot_general(
-        placing, input_grad, contract_rows, preferred_element_type=jnp.float32
-    )
-    normed_grad = joined_grad.astype(jnp.float32) + mixture_grad
+    input_grad = shard_partials(grad_pre, full_in.T, shards)
+    row_normed_grad = joined_grad.astype(jnp.float32) + input_grad.astype(jnp.float32)
+    back = jnp.concatenate(
+        [
+            row_normed_grad,
+            predicted,
+            jnp.zeros((local_rows, lanes - width - 3), jnp.float32),
+        ],
+        axis=1,
+    )
+    mine = jnp.take(to_owners(back, owners), target_slot, axis=0)
+    normed_grad = mine[:, :width]
+    predicted = mine[:, width : width + 3]
     scaled_grad = normed_grad * norm_gain
     summed_grad = inverse * (
         scaled_grad

time: 427 us -> 409 us (0.958)
  the two profiles are of different devices: /device:TPU:40 before, /device:TPU:8 now
where the time goes in v3:
time: 409 us; the launch traced here: 408 us
  waiting for transfers between devices  261 us (64%)
  starting transfers between devices  58.1 us (14%)
  matrix products  38.6 us (9%)
  other arithmetic  22.3 us (5%)
  between operations  14.2 us (3%)
  local copies, waits for them, and re-layouts  14.1 us (3%)
    all_to_all x1, waiting for transfers between devices, step(): lax.all_to_all(pooled.reshape(owners, samples, pooled.shape[-1]), 'table'...  121 us
    all_to_all x1, waiting for transfers between devices, step(): lax.all_to_all(feature_grad, 'table', split_axis=0, concat_axis=0, tiled=...  52.4 us
    all_to_all x2, starting transfers between devices, to_owners(): lax.all_to_all(shaped, 'table', split_axis=0, concat_axis=0, tiled=True)  30 us
    all_gather x1, waiting for transfers between devices, step(): all_rows = lax.all_gather(rows, 'expert', axis=0, tiled=True)  28.4 us
    all_gather x1, waiting for transfers between devices, step(): all_grads = lax.all_gather(row_grads, 'expert', axis=0, tiled=True)  27.1 us
    all_to_all x2, waiting for transfers between devices, to_owners(): lax.all_to_all(shaped, 'table', split_axis=0, concat_axis=0, tiled=True)  24 us
    all_to_all x1, starting transfers between devices, step(): lax.all_to_all(pooled.reshape(owners, samples, pooled.shape[-1]), 'table'...  16.9 us
    reduce_sum x1, other arithmetic, bag_counts_t(): return jnp.sum(hits, axis=0).astype(jnp.bfloat16)  11.3 us
  transfers between devices with their start and end apart: 9, of which 7 were waited for; matrix products, arithmetic and copies ran while one was open for 7% of the time, Pallas kernels for 0%

profile of v3, /device:TPU:8, one launch (start us, length us, event | category | flops | bytes accessed | tf_op | source)
XLA Modules:
  0.0 408.1 jit_solution(3977929752582541874)
XLA Ops:
  7.2 1.0 bitcast_select_fusion
  8.3 11.3 %convert_reduce_fusion = bf16[256,8192]{1,0:T(8,128)(2,1)} fusion(s32[8,8192]{1,0:T(8,128)S(1)} %bitcast_select_fusion), kind=kLoop, calls=%fused_computation.4 | loop fusion | flops 48234496 | bytes 4456448 | tf_op jit(solution)/shard_map/reduce_sum | solution.py:20
  19.5 1.9 gather_fusion.1
  21.5 1.2 gather_fusion
  22.7 5.6 %convolution_convert_fusion = bf16[8192,256]{1,0:T(8,128)(2,1)} fusion(bf16[256,8192]{1,0:T(8,128)(2,1)} %convert_reduce_fusion, f32[256]{0:T(256)S(1)} %get-tuple-element.34, bf16[256,256]{1,0:T(8,128)(2,1)S(1)} %gather_fusion, pred[256]{0:T(512)(128)(4,1)S(1)} %get-tuple-element.35), kind=kOutput, calls=%fused_computation.6 | convolution fusion | flops 1076166656 | bytes 8520960 | tf_op jit(solution)/shard_map/dot_general | solution.py:69
  28.2 16.9 %all-to-all-start = ((bf16[64,128,256]{2,1,0:T(8,128)(2,1)}), bf16[64,128,256]{2,1,0:T(8,128)(2,1)}, u32[]{:S(2)}, u32[]{:S(2)}) async-start(bf16[64,128,256]{2,1,0:T(8,128)(2,1)} %bitcast.102), calls=%async_computation | async-start | bytes 8388608 | tf_op jit(solution)/shard_map/all_to_all | solution.py:72
  47.7 121.2 %all-to-all-done = bf16[64,128,256]{2,1,0:T(8,128)(2,1)} async-done(((bf16[64,128,256]{2,1,0:T(8,128)(2,1)}), bf16[64,128,256]{2,1,0:T(8,128)(2,1)}, u32[]{:S(2)}, u32[]{:S(2)}) %all-to-all-start) | async-done | bytes 4194336 | tf_op jit(solution)/shard_map/all_to_all | solution.py:72
  168.9 3.1 multiply_reduce_fusion
  172.3 1.0 gather_fusion.2
  173.4 0.9 broadcast_select_fusion
  174.3 23.7 %all-to-all-start.1 = ((f32[64,4,384]{2,1,0:T(4,128)}), f32[64,4,384]{2,1,0:T(4,128)S(1)}, u32[]{:S(2)}, u32[]{:S(2)}) async-start(f32[64,4,384]{2,1,0:T(4,128)} %broadcast_select_fusion), calls=%async_computation.1 | async-start | bytes 786432 | tf_op jit(solution)/shard_map/all_to_all | solution.py:25
  198.1 4.2 %copy.78 = bf16[4096,256]{1,0:T(8,128)(2,1)} copy(bf16[4096,256]{0,1:T(8,128)(2,1)} %bitcast.104) | data formatting | bytes 4194304 | tf_op jit(solution)/shard_map/transpose | solution.py:131
  202.3 9.6 %all-to-all-done.1 = f32[64,4,384]{2,1,0:T(4,128)S(1)} async-done(((f32[64,4,384]{2,1,0:T(4,128)}), f32[64,4,384]{2,1,0:T(4,128)S(1)}, u32[]{:S(2)}, u32[]{:S(2)}) %all-to-all-start.1) | async-done | bytes 393248 | tf_op jit(solution)/shard_map/all_to_all | solution.py:25
  212.4 4.0 multiply_convert_fusion.3
  216.3 2.9 fusion.24
  221.6 4.7 %fusion = bf16[256,4096]{1,0:T(8,128)(2,1)S(1)} fusion(bf16[256,256]{1,0:T(8,128)(2,1)S(1)} %fusion.29, f32[256,4096]{1,0:T(8,128)} %get-tuple-element.43, bf16[1,4096,256]{2,1,0:T(8,128)(2,1)} %all-gather.13.cloned.1.call-done), kind=kOutput, calls=%fused_computation.10 | convolution fusion | flops 546308096 | bytes 8519680 | tf_op jit(solution)/shard_map/dot_general | solution.py:127
  228.0 1.2 concatenate.19
  229.2 6.3 %all-to-all-start.2 = ((f32[64,4,384]{2,1,0:T(4,128)}), f32[64,4,384]{2,1,0:T(4,128)S(1)}, u32[]{:S(2)}, u32[]{:S(2)}) async-start(f32[64,4,384]{2,1,0:T(4,128)} %concatenate.19), calls=%async_computation.2 | async-start | bytes 786432 | tf_op jit(solution)/shard_map/all_to_all | solution.py:25
  235.5 14.3 %all-to-all-done.2 = f32[64,4,384]{2,1,0:T(4,128)S(1)} async-done(((f32[64,4,384]{2,1,0:T(4,128)}), f32[64,4,384]{2,1,0:T(4,128)S(1)}, u32[]{:S(2)}, u32[]{:S(2)}) %all-to-all-start.2) | async-done | bytes 393248 | tf_op jit(solution)/shard_map/all_to_all | solution.py:25
  250.0 0.8 gather_fusion.3
  251.1 3.4 multiply_convert_fusion
  254.5 7.3 %all-to-all-start.3 = ((bf16[64,128,256]{2,1,0:T(8,128)(2,1)}), bf16[64,128,256]{2,1,0:T(8,128)(2,1)}, u32[]{:S(2)}, u32[]{:S(2)}) async-start(bf16[64,128,256]{2,1,0:T(8,128)(2,1)} %multiply_convert_fusion), calls=%async_computation.3 | async-start | bytes 8388608 | tf_op jit(solution)/shard_map/all_to_all | solution.py:150
  263.8 28.4 %all-gather.7.cloned.1.call-done = bf16[2048,256]{1,0:T(8,128)(2,1)} async-done(((bf16[256,256]{1,0:T(8,128)(2,1)}), bf16[2048,256]{1,0:T(8,128)(2,1)}) %all-gather.7.cloned.1.call-update) | async-done | bytes 1048592 | tf_op jit(solution)/shard_map/all_gather | solution.py:108
  292.2 4.0 fusion.31
  296.2 27.1 %all-gather.9.cloned.1.call-done = bf16[2048,256]{1,0:T(8,128)(2,1)} async-done(((bf16[256,256]{1,0:T(8,128)(2,1)}), bf16[2048,256]{1,0:T(8,128)(2,1)}) %all-gather.9.cloned.1.call-update) | async-done | bytes 1048592 | tf_op jit(solution)/shard_map/all_gather | solution.py:126
  323.3 5.4 %fusion.27 = f32[1,256,512]{2,1,0:T(8,128)} fusion(bf16[2048,256]{1,0:T(8,128)(2,1)S(1)} %copy-done.3, f32[2048,512]{1,0:T(8,128)} %fusion.31, bf16[2048,256]{1,0:T(8,128)(2,1)} %all-gather.9.cloned.1.call-done, bf16[1,512,256]{2,1,0:T(8,128)(2,1)S(1)} %copy-done.9), kind=kOutput, calls=%fused_computation.35 | convolution fusion | flops 1083179008 | bytes 7077888 | tf_op jit(solution)/shard_map/dot_general | solution.py:177
  328.8 52.4 %all-to-all-done.3 = bf16[64,128,256]{2,1,0:T(8,128)(2,1)} async-done(((bf16[64,128,256]{2,1,0:T(8,128)(2,1)}), bf16[64,128,256]{2,1,0:T(8,128)(2,1)}, u32[]{:S(2)}, u32[]{:S(2)}) %all-to-all-start.3) | async-done | bytes 4194336 | tf_op jit(solution)/shard_map/all_to_all | solution.py:150
  381.2 4.8 %fusion.65 = f32[256,256]{1,0:T(8,128)S(1)} fusion(bf16[256,8192]{1,0:T(8,128)(2,1)} %convert_reduce_fusion, bf16[8192,256]{1,0:T(8,128)(2,1)} %bitcast.29), kind=kOutput, calls=%fused_computation.117 | convolution fusion | flops 1073741824 | bytes 8650752 | tf_op jit(solution)/shard_map/dot_general | solution.py:153
  385.9 1.2 fusion.30
  387.2 3.5 all-to-all-start.4
  390.7 4.3 %fusion.28 = f32[1,512,256]{2,1,0:T(8,128)} fusion(bf16[2048,256]{1,0:T(8,128)(2,1)S(1)} %copy-done.14, f32[2048,512]{1,0:T(8,128)} %fusion.31), kind=kOutput, calls=%fused_computation.36 | convolution fusion | flops 542113792 | bytes 5767168 | tf_op jit(solution)/shard_map/dot_general | solution.py:174
  395.0 6.0 %all-to-all-done.4 = f32[8,64,256]{2,1,0:T(8,128)S(1)} async-done(((f32[8,64,256]{2,1,0:T(8,128)}), f32[8,64,256]{2,1,0:T(8,128)S(1)}, u32[]{:S(2)}, u32[]{:S(2)}) %all-to-all-start.4) | async-done | bytes 524320 | tf_op jit(solution)/shard_map/all_to_all | solution.py:159
  (92 shorter events, 10.2 us)
Async XLA Ops:
  7.2 212.1 %copy-start = (bf16[3,256,256]{2,1,0:T(8,128)(2,1)S(1)}, bf16[3,256,256]{2,1,0:T(8,128)(2,1)}, u32[]{:S(2)}) copy-start(bf16[3,256,256]{2,1,0:T(8,128)(2,1)} %param.23) | copy-start | bytes 1179652
  7.2 12.3 %copy-start.11 = (s32[1,1,256]{2,1,0:T(1,128)S(1)}, s32[1,1,256]{2,1,0:T(1,128)}, u32[]{:S(2)}) copy-start(s32[1,1,256]{2,1,0:T(1,128)} %param.15) | copy-start | bytes 3076
  7.2 12.3 %copy-start.1 = (f32[1,512]{1,0:T(1,128)S(1)}, f32[1,512]{1,0:T(1,128)}, u32[]{:S(2)}) copy-start(f32[1,512]{1,0:T(1,128)} %param.14) | copy-start | bytes 6148
  7.2 14.3 %copy-start.2 = (bf16[1,512,256]{2,1,0:T(8,128)(2,1)S(1)}, bf16[1,512,256]{2,1,0:T(8,128)(2,1)}, u32[]{:S(2)}) copy-start(bf16[1,512,256]{2,1,0:T(8,128)(2,1)} %param.13) | copy-start | bytes 786436
  28.2 18.4 %copy-start.13 = (f32[1,128,3]{1,0,2:T(1,128)S(1)}, f32[1,128,3]{1,0,2:T(1,128)}, u32[]{:S(2)}) copy-start(f32[1,128,3]{1,0,2:T(1,128)} %param.25) | copy-start | bytes 4612
  28.2 18.7 %copy-start.12 = (s32[1,128,1]{1,2,0:T(1,128)S(1)}, s32[1,128,1]{1,2,0:T(1,128)}, u32[]{:S(2)}) copy-start(s32[1,128,1]{1,2,0:T(1,128)} %param.20) | copy-start | bytes 1540
  28.2 140.7 %copy-start.8 = (f32[64,256]{1,0:T(8,128)S(1)}, f32[64,256]{1,0:T(8,128)}, u32[]{:S(2)}) copy-start(f32[64,256]{1,0:T(8,128)} %param.18) | copy-start | bytes 196612
  28.2 140.7 %all-to-all-start = ((bf16[64,128,256]{2,1,0:T(8,128)(2,1)}), bf16[64,128,256]{2,1,0:T(8,128)(2,1)}, u32[]{:S(2)}, u32[]{:S(2)}) async-start(bf16[64,128,256]{2,1,0:T(8,128)(2,1)} %bitcast.102), calls=%async_computation | async-start | bytes 8388608 | tf_op jit(solution)/shard_map/all_to_all | solution.py:72
  45.1 127.0 %copy-start.10 = (f32[256]{0:T(256)S(1)}, f32[256]{0:T(256)}, u32[]{:S(2)}) copy-start(f32[256]{0:T(256)} %param.19) | copy-start | bytes 3076
  45.2 152.9 %all-gather.11.cloned.1.call-start = ((), (), s32[]{:S(2)}) async-start(), calls=%async_computation.7 | async-start | bytes 2359296 | tf_op jit(solution)/shard_map/all_gather | solution.py:60
  45.9 170.4 %all-gather.13.cloned.1.call-start = ((), (), s32[]{:S(2)}) async-start(), calls=%async_computation.8 | async-start | bytes 2359296 | tf_op jit(solution)/shard_map/all_gather | solution.py:61
  174.3 37.6 %all-to-all-start.1 = ((f32[64,4,384]{2,1,0:T(4,128)}), f32[64,4,384]{2,1,0:T(4,128)S(1)}, u32[]{:S(2)}, u32[]{:S(2)}) async-start(f32[64,4,384]{2,1,0:T(4,128)} %broadcast_select_fusion), calls=%async_computation.1 | async-start | bytes 786432 | tf_op jit(solution)/shard_map/all_to_all | solution.py:25
  198.1 14.3 %copy-start.4 = (bf16[1,256,4096]{2,1,0:T(8,128)(2,1)S(1)}, bf16[1,256,4096]{2,1,0:T(8,128)(2,1)}, u32[]{:S(2)}) copy-start(bf16[1,256,4096]{2,1,0:T(8,128)(2,1)} %all-gather.11.cloned.1.call-done) | copy-start | bytes 6291460
  216.3 3.0 copy-start.15
  221.5 5.5 %copy-start.7 = (bf16[256,256]{1,0:T(8,128)(2,1)}, bf16[256,256]{1,0:T(8,128)(2,1)S(1)}, u32[]{:S(2)}) copy-start(bf16[256,256]{1,0:T(8,128)(2,1)S(1)} %fusion.29) | copy-start | bytes 393220
  221.5 4.7 %copy-start.5 = (bf16[4096,256]{1,0:T(8,128)(2,1)S(1)}, bf16[4096,256]{1,0:T(8,128)(2,1)}, u32[]{:S(2)}) copy-start(bf16[4096,256]{1,0:T(8,128)(2,1)} %copy.78) | copy-start | bytes 6291460
  229.2 20.6 %all-to-all-start.2 = ((f32[64,4,384]{2,1,0:T(4,128)}), f32[64,4,384]{2,1,0:T(4,128)S(1)}, u32[]{:S(2)}, u32[]{:S(2)}) async-start(f32[64,4,384]{2,1,0:T(4,128)} %concatenate.19), calls=%async_computation.2 | async-start | bytes 786432 | tf_op jit(solution)/shard_map/all_to_all | solution.py:25
  254.5 37.7 %copy-start.6 = (bf16[1,256,512]{2,1,0:T(8,128)(2,1)S(1)}, bf16[1,256,512]{2,1,0:T(8,128)(2,1)}, u32[]{:S(2)}) copy-start(bf16[1,256,512]{2,1,0:T(8,128)(2,1)} %param.21) | copy-start | bytes 786436
  254.5 126.7 %all-to-all-start.3 = ((bf16[64,128,256]{2,1,0:T(8,128)(2,1)}), bf16[64,128,256]{2,1,0:T(8,128)(2,1)}, u32[]{:S(2)}, u32[]{:S(2)}) async-start(bf16[64,128,256]{2,1,0:T(8,128)(2,1)} %multiply_convert_fusion), calls=%async_computation.3 | async-start | bytes 8388608 | tf_op jit(solution)/shard_map/all_to_all | solution.py:150
  261.8 30.4 %all-gather.7.cloned.1.call-start = ((), (), s32[]{:S(2)}) async-start(), calls=%async_computation.5 | async-start | bytes 1179648 | tf_op jit(solution)/shard_map/all_gather | solution.py:108
  262.5 60.8 %all-gather.9.cloned.1.call-start = ((), (), s32[]{:S(2)}) async-start(), calls=%async_computation.6 | async-start | bytes 1179648 | tf_op jit(solution)/shard_map/all_gather | solution.py:126
  263.8 59.5 %copy-start.9 = (bf16[1,512,256]{2,1,0:T(8,128)(2,1)S(1)}, bf16[1,512,256]{2,1,0:T(8,128)(2,1)}, u32[]{:S(2)}) copy-start(bf16[1,512,256]{2,1,0:T(8,128)(2,1)} %param.22) | copy-start | bytes 786436
  292.2 31.1 %copy-start.3 = (bf16[2048,256]{1,0:T(8,128)(2,1)S(1)}, bf16[2048,256]{1,0:T(8,128)(2,1)}, u32[]{:S(2)}) copy-start(bf16[2048,256]{1,0:T(8,128)(2,1)} %all-gather.7.cloned.1.call-done) | copy-start | bytes 3145732
  381.2 9.5 %copy-start.14 = (bf16[2048,256]{1,0:T(8,128)(2,1)S(1)}, bf16[2048,256]{1,0:T(8,128)(2,1)}, u32[]{:S(2)}) copy-start(bf16[2048,256]{1,0:T(8,128)(2,1)} %all-gather.9.cloned.1.call-done) | copy-start | bytes 3145732
  387.2 13.7 %all-to-all-start.4 = ((f32[8,64,256]{2,1,0:T(8,128)}), f32[8,64,256]{2,1,0:T(8,128)S(1)}, u32[]{:S(2)}, u32[]{:S(2)}) async-start(f32[8,64,256]{2,1,0:T(8,128)} %bitcast.30), calls=%async_computation.4 | async-start | bytes 1048576 | tf_op jit(solution)/shard_map/all_to_all | solution.py:159
Sparse Core Ops, SparseCore 0:
  48.1 31.2 all-gather.10
  81.6 30.9 all-gather.12
  265.3 26.8 all-gather.6
  294.8 28.4 all-gather.8

commit v4 on v3

--- a/solution.py
+++ b/solution.py
@@ -14,10 +14,10 @@
 
 def bag_counts_t(indices, lengths, window):
     slots = jnp.arange(indices.shape[1], dtype=jnp.int32)
-    live = jnp.where(slots[:, None] < lengths[None, :], indices.T, -1)
-    positions = jnp.arange(window, dtype=jnp.int32)
-    hits = (live[:, None, :] == positions[None, :, None]).astype(jnp.float32)
-    return jnp.sum(hits, axis=0).astype(jnp.bfloat16)
+    live = jnp.where(slots[:, None] < lengths[None, :], indices.T, -1).astype(jnp.bfloat16)
+    positions = jnp.arange(window, dtype=jnp.int32).astype(jnp.bfloat16)
+    hits = (live[:, None, :] == positions[None, :, None]).astype(jnp.bfloat16)
+    return jnp.sum(hits, axis=0, dtype=jnp.bfloat16)
 
 
 def to_owners(rows, owners):

time: 409 us -> 418 us (1.022)
  the two profiles are of different devices: /device:TPU:8 before, /device:TPU:216 now
where the time goes in v4:
time: 418 us; the launch traced here: 417 us
  waiting for transfers between devices  269 us (64%)
  starting transfers between devices  57.7 us (14%)
  matrix products  38.6 us (9%)
  other arithmetic  22.9 us (5%)
  local copies, waits for them, and re-layouts  15 us (4%)
  between operations  14.2 us (3%)
    all_to_all x1, waiting for transfers between devices, step(): lax.all_to_all(pooled.reshape(owners, samples, pooled.shape[-1]), 'table'...  124 us
    all_to_all x1, waiting for transfers between devices, step(): lax.all_to_all(feature_grad, 'table', split_axis=0, concat_axis=0, tiled=...  60 us
    all_gather x1, waiting for transfers between devices, step(): all_rows = lax.all_gather(rows, 'expert', axis=0, tiled=True)  31 us
    all_to_all x2, starting transfers between devices, to_owners(): lax.all_to_all(shaped, 'table', split_axis=0, concat_axis=0, tiled=True)  29.9 us
    all_gather x1, waiting for transfers between devices, step(): all_grads = lax.all_gather(row_grads, 'expert', axis=0, tiled=True)  27.1 us
    all_to_all x2, waiting for transfers between devices, to_owners(): lax.all_to_all(shaped, 'table', split_axis=0, concat_axis=0, tiled=True)  19.3 us
    all_to_all x1, starting transfers between devices, step(): lax.all_to_all(pooled.reshape(owners, samples, pooled.shape[-1]), 'table'...  14 us
    reduce_sum x1, other arithmetic, bag_counts_t(): return jnp.sum(hits, axis=0, dtype=jnp.bfloat16)  11.3 us
  transfers between devices with their start and end apart: 9, of which 7 were waited for; matrix products, arithmetic and copies ran while one was open for 7% of the time, Pallas kernels for 0%

profile of v4, /device:TPU:216, one launch (start us, length us, event | category | flops | bytes accessed | tf_op | source)
XLA Modules:
  0.0 417.0 jit_solution(11029776199504671714)
XLA Ops:
  7.9 2.0 gather_fusion.1
  9.9 2.0 gather_fusion
  11.9 1.0 fusion.29
  12.9 11.3 %fusion = bf16[256,8192]{1,0:T(8,128)(2,1)} fusion(bf16[8,8192]{1,0:T(8,128)(2,1)S(1)} %fusion.29, bf16[256]{0:T(256)(128)(2,1)S(1)} %iota_convert_fusion), kind=kLoop, calls=%fused_computation.5 | loop fusion | flops 48234496 | bytes 4325888 | tf_op jit(solution)/shard_map/reduce_sum | solution.py:20
  24.2 5.6 %convolution_convert_fusion = bf16[8192,256]{1,0:T(8,128)(2,1)} fusion(bf16[256,8192]{1,0:T(8,128)(2,1)} %fusion, f32[256]{0:T(256)S(1)} %get-tuple-element.34, bf16[256,256]{1,0:T(8,128)(2,1)S(1)} %gather_fusion, pred[256]{0:T(512)(128)(4,1)S(1)} %get-tuple-element.35), kind=kOutput, calls=%fused_computation.6 | convolution fusion | flops 1076166656 | bytes 8520960 | tf_op jit(solution)/shard_map/dot_general | solution.py:69
  29.7 14.0 %all-to-all-start = ((bf16[64,128,256]{2,1,0:T(8,128)(2,1)}), bf16[64,128,256]{2,1,0:T(8,128)(2,1)}, u32[]{:S(2)}, u32[]{:S(2)}) async-start(bf16[64,128,256]{2,1,0:T(8,128)(2,1)} %bitcast.104), calls=%async_computation | async-start | bytes 8388608 | tf_op jit(solution)/shard_map/all_to_all | solution.py:72
  46.3 123.5 %all-to-all-done = bf16[64,128,256]{2,1,0:T(8,128)(2,1)} async-done(((bf16[64,128,256]{2,1,0:T(8,128)(2,1)}), bf16[64,128,256]{2,1,0:T(8,128)(2,1)}, u32[]{:S(2)}, u32[]{:S(2)}) %all-to-all-start) | async-done | bytes 4194336 | tf_op jit(solution)/shard_map/all_to_all | solution.py:72
  169.8 3.1 multiply_reduce_fusion
  173.2 1.0 gather_fusion.2
  174.3 0.9 broadcast_select_fusion
  175.2 21.1 %all-to-all-start.1 = ((f32[64,4,384]{2,1,0:T(4,128)}), f32[64,4,384]{2,1,0:T(4,128)S(1)}, u32[]{:S(2)}, u32[]{:S(2)}) async-start(f32[64,4,384]{2,1,0:T(4,128)} %broadcast_select_fusion), calls=%async_computation.1 | async-start | bytes 786432 | tf_op jit(solution)/shard_map/all_to_all | solution.py:25
  196.3 4.2 %copy.78 = bf16[4096,256]{1,0:T(8,128)(2,1)} copy(bf16[4096,256]{0,1:T(8,128)(2,1)} %bitcast.106) | data formatting | bytes 4194304 | tf_op jit(solution)/shard_map/transpose | solution.py:131
  200.6 7.5 %all-to-all-done.1 = f32[64,4,384]{2,1,0:T(4,128)S(1)} async-done(((f32[64,4,384]{2,1,0:T(4,128)}), f32[64,4,384]{2,1,0:T(4,128)S(1)}, u32[]{:S(2)}, u32[]{:S(2)}) %all-to-all-start.1) | async-done | bytes 393248 | tf_op jit(solution)/shard_map/all_to_all | solution.py:25
  208.5 4.0 multiply_convert_fusion.3
  212.5 2.9 fusion.22
  217.7 4.7 %fusion.1 = bf16[256,4096]{1,0:T(8,128)(2,1)S(1)} fusion(bf16[256,256]{1,0:T(8,128)(2,1)S(1)} %fusion.27, f32[256,4096]{1,0:T(8,128)} %get-tuple-element.43, bf16[1,4096,256]{2,1,0:T(8,128)(2,1)} %all-gather.13.cloned.1.call-done), kind=kOutput, calls=%fused_computation.10 | convolution fusion | flops 546308096 | bytes 8519680 | tf_op jit(solution)/shard_map/dot_general | solution.py:127
  224.1 1.2 concatenate.19
  225.4 8.8 %all-to-all-start.2 = ((f32[64,4,384]{2,1,0:T(4,128)}), f32[64,4,384]{2,1,0:T(4,128)S(1)}, u32[]{:S(2)}, u32[]{:S(2)}) async-start(f32[64,4,384]{2,1,0:T(4,128)} %concatenate.19), calls=%async_computation.2 | async-start | bytes 786432 | tf_op jit(solution)/shard_map/all_to_all | solution.py:25
  234.2 11.8 %all-to-all-done.2 = f32[64,4,384]{2,1,0:T(4,128)S(1)} async-done(((f32[64,4,384]{2,1,0:T(4,128)}), f32[64,4,384]{2,1,0:T(4,128)S(1)}, u32[]{:S(2)}, u32[]{:S(2)}) %all-to-all-start.2) | async-done | bytes 393248 | tf_op jit(solution)/shard_map/all_to_all | solution.py:25
  246.1 0.8 gather_fusion.3
  247.2 3.4 multiply_convert_fusion
  250.6 9.8 %all-to-all-start.3 = ((bf16[64,128,256]{2,1,0:T(8,128)(2,1)}), bf16[64,128,256]{2,1,0:T(8,128)(2,1)}, u32[]{:S(2)}, u32[]{:S(2)}) async-start(bf16[64,128,256]{2,1,0:T(8,128)(2,1)} %multiply_convert_fusion), calls=%async_computation.3 | async-start | bytes 8388608 | tf_op jit(solution)/shard_map/all_to_all | solution.py:150
  262.5 31.0 %all-gather.7.cloned.1.call-done = bf16[2048,256]{1,0:T(8,128)(2,1)} async-done(((bf16[256,256]{1,0:T(8,128)(2,1)}), bf16[2048,256]{1,0:T(8,128)(2,1)}) %all-gather.7.cloned.1.call-update) | async-done | bytes 1048592 | tf_op jit(solution)/shard_map/all_gather | solution.py:108
  293.5 4.0 fusion.30
  297.5 27.1 %all-gather.9.cloned.1.call-done = bf16[2048,256]{1,0:T(8,128)(2,1)} async-done(((bf16[256,256]{1,0:T(8,128)(2,1)}), bf16[2048,256]{1,0:T(8,128)(2,1)}) %all-gather.9.cloned.1.call-update) | async-done | bytes 1048592 | tf_op jit(solution)/shard_map/all_gather | solution.py:126
  324.6 5.4 %fusion.25 = f32[1,256,512]{2,1,0:T(8,128)} fusion(bf16[2048,256]{1,0:T(8,128)(2,1)S(1)} %copy-done.1, f32[2048,512]{1,0:T(8,128)} %fusion.30, bf16[2048,256]{1,0:T(8,128)(2,1)} %all-gather.9.cloned.1.call-done, bf16[1,512,256]{2,1,0:T(8,128)(2,1)S(1)} %copy-done.7), kind=kOutput, calls=%fused_computation.32 | convolution fusion | flops 1083179008 | bytes 7077888 | tf_op jit(solution)/shard_map/dot_general | solution.py:177
  330.0 60.0 %all-to-all-done.3 = bf16[64,128,256]{2,1,0:T(8,128)(2,1)} async-done(((bf16[64,128,256]{2,1,0:T(8,128)(2,1)}), bf16[64,128,256]{2,1,0:T(8,128)(2,1)}, u32[]{:S(2)}, u32[]{:S(2)}) %all-to-all-start.3) | async-done | bytes 4194336 | tf_op jit(solution)/shard_map/all_to_all | solution.py:150
  390.1 4.8 %fusion.64 = f32[256,256]{1,0:T(8,128)S(1)} fusion(bf16[256,8192]{1,0:T(8,128)(2,1)} %fusion, bf16[8192,256]{1,0:T(8,128)(2,1)} %bitcast.29), kind=kOutput, calls=%fused_computation.116 | convolution fusion | flops 1073741824 | bytes 8650752 | tf_op jit(solution)/shard_map/dot_general | solution.py:153
  394.9 1.2 fusion.28
  396.1 3.5 all-to-all-start.4
  399.6 4.3 %fusion.26 = f32[1,512,256]{2,1,0:T(8,128)} fusion(bf16[2048,256]{1,0:T(8,128)(2,1)S(1)} %copy-done.12, f32[2048,512]{1,0:T(8,128)} %fusion.30), kind=kOutput, calls=%fused_computation.33 | convolution fusion | flops 542113792 | bytes 5767168 | tf_op jit(solution)/shard_map/dot_general | solution.py:174
  403.9 6.0 %all-to-all-done.4 = f32[8,64,256]{2,1,0:T(8,128)S(1)} async-done(((f32[8,64,256]{2,1,0:T(8,128)}), f32[8,64,256]{2,1,0:T(8,128)S(1)}, u32[]{:S(2)}, u32[]{:S(2)}) %all-to-all-start.4) | async-done | bytes 524320 | tf_op jit(solution)/shard_map/all_to_all | solution.py:159
  (89 shorter events, 10.9 us)
Async XLA Ops:
  7.2 208.3 %copy-start = (bf16[3,256,256]{2,1,0:T(8,128)(2,1)S(1)}, bf16[3,256,256]{2,1,0:T(8,128)(2,1)}, u32[]{:S(2)}) copy-start(bf16[3,256,256]{2,1,0:T(8,128)(2,1)} %param.23) | copy-start | bytes 1179652
  7.2 17.0 %copy-start.9 = (s32[1,1,256]{2,1,0:T(1,128)S(1)}, s32[1,1,256]{2,1,0:T(1,128)}, u32[]{:S(2)}) copy-start(s32[1,1,256]{2,1,0:T(1,128)} %param.15) | copy-start | bytes 3076
  29.7 15.5 %copy-start.11 = (f32[1,128,3]{1,0,2:T(1,128)S(1)}, f32[1,128,3]{1,0,2:T(1,128)}, u32[]{:S(2)}) copy-start(f32[1,128,3]{1,0,2:T(1,128)} %param.25) | copy-start | bytes 4612
  29.7 15.8 %copy-start.10 = (s32[1,128,1]{1,2,0:T(1,128)S(1)}, s32[1,128,1]{1,2,0:T(1,128)}, u32[]{:S(2)}) copy-start(s32[1,128,1]{1,2,0:T(1,128)} %param.20) | copy-start | bytes 1540
  29.7 140.0 %copy-start.6 = (f32[64,256]{1,0:T(8,128)S(1)}, f32[64,256]{1,0:T(8,128)}, u32[]{:S(2)}) copy-start(f32[64,256]{1,0:T(8,128)} %param.18) | copy-start | bytes 196612
  29.7 140.0 %all-to-all-start = ((bf16[64,128,256]{2,1,0:T(8,128)(2,1)}), bf16[64,128,256]{2,1,0:T(8,128)(2,1)}, u32[]{:S(2)}, u32[]{:S(2)}) async-start(bf16[64,128,256]{2,1,0:T(8,128)(2,1)} %bitcast.104), calls=%async_computation | async-start | bytes 8388608 | tf_op jit(solution)/shard_map/all_to_all | solution.py:72
  43.7 129.3 %copy-start.8 = (f32[256]{0:T(256)S(1)}, f32[256]{0:T(256)}, u32[]{:S(2)}) copy-start(f32[256]{0:T(256)} %param.19) | copy-start | bytes 3076
  43.8 152.6 %all-gather.11.cloned.1.call-start = ((), (), s32[]{:S(2)}) async-start(), calls=%async_computation.7 | async-start | bytes 2359296 | tf_op jit(solution)/shard_map/all_gather | solution.py:60
  44.5 168.0 %all-gather.13.cloned.1.call-start = ((), (), s32[]{:S(2)}) async-start(), calls=%async_computation.8 | async-start | bytes 2359296 | tf_op jit(solution)/shard_map/all_gather | solution.py:61
  175.2 32.9 %all-to-all-start.1 = ((f32[64,4,384]{2,1,0:T(4,128)}), f32[64,4,384]{2,1,0:T(4,128)S(1)}, u32[]{:S(2)}, u32[]{:S(2)}) async-start(f32[64,4,384]{2,1,0:T(4,128)} %broadcast_select_fusion), calls=%async_computation.1 | async-start | bytes 786432 | tf_op jit(solution)/shard_map/all_to_all | solution.py:25
  196.3 12.2 %copy-start.2 = (bf16[1,256,4096]{2,1,0:T(8,128)(2,1)S(1)}, bf16[1,256,4096]{2,1,0:T(8,128)(2,1)}, u32[]{:S(2)}) copy-start(bf16[1,256,4096]{2,1,0:T(8,128)(2,1)} %all-gather.11.cloned.1.call-done) | copy-start | bytes 6291460
  212.5 3.0 copy-start.13
  217.7 5.5 %copy-start.5 = (bf16[256,256]{1,0:T(8,128)(2,1)}, bf16[256,256]{1,0:T(8,128)(2,1)S(1)}, u32[]{:S(2)}) copy-start(bf16[256,256]{1,0:T(8,128)(2,1)S(1)} %fusion.27) | copy-start | bytes 393220
  217.7 4.7 %copy-start.3 = (bf16[4096,256]{1,0:T(8,128)(2,1)S(1)}, bf16[4096,256]{1,0:T(8,128)(2,1)}, u32[]{:S(2)}) copy-start(bf16[4096,256]{1,0:T(8,128)(2,1)} %copy.78) | copy-start | bytes 6291460
  225.4 20.6 %all-to-all-start.2 = ((f32[64,4,384]{2,1,0:T(4,128)}), f32[64,4,384]{2,1,0:T(4,128)S(1)}, u32[]{:S(2)}, u32[]{:S(2)}) async-start(f32[64,4,384]{2,1,0:T(4,128)} %concatenate.19), calls=%async_computation.2 | async-start | bytes 786432 | tf_op jit(solution)/shard_map/all_to_all | solution.py:25
  250.6 42.9 %copy-start.4 = (bf16[1,256,512]{2,1,0:T(8,128)(2,1)S(1)}, bf16[1,256,512]{2,1,0:T(8,128)(2,1)}, u32[]{:S(2)}) copy-start(bf16[1,256,512]{2,1,0:T(8,128)(2,1)} %param.21) | copy-start | bytes 786436
  250.6 139.4 %all-to-all-start.3 = ((bf16[64,128,256]{2,1,0:T(8,128)(2,1)}), bf16[64,128,256]{2,1,0:T(8,128)(2,1)}, u32[]{:S(2)}, u32[]{:S(2)}) async-start(bf16[64,128,256]{2,1,0:T(8,128)(2,1)} %multiply_convert_fusion), calls=%async_computation.3 | async-start | bytes 8388608 | tf_op jit(solution)/shard_map/all_to_all | solution.py:150
  260.5 33.0 %all-gather.7.cloned.1.call-start = ((), (), s32[]{:S(2)}) async-start(), calls=%async_computation.5 | async-start | bytes 1179648 | tf_op jit(solution)/shard_map/all_gather | solution.py:108
  261.2 63.4 %all-gather.9.cloned.1.call-start = ((), (), s32[]{:S(2)}) async-start(), calls=%async_computation.6 | async-start | bytes 1179648 | tf_op jit(solution)/shard_map/all_gather | solution.py:126
  262.5 62.1 %copy-start.7 = (bf16[1,512,256]{2,1,0:T(8,128)(2,1)S(1)}, bf16[1,512,256]{2,1,0:T(8,128)(2,1)}, u32[]{:S(2)}) copy-start(bf16[1,512,256]{2,1,0:T(8,128)(2,1)} %param.22) | copy-start | bytes 786436
  293.5 31.1 %copy-start.1 = (bf16[2048,256]{1,0:T(8,128)(2,1)S(1)}, bf16[2048,256]{1,0:T(8,128)(2,1)}, u32[]{:S(2)}) copy-start(bf16[2048,256]{1,0:T(8,128)(2,1)} %all-gather.7.cloned.1.call-done) | copy-start | bytes 3145732
  390.1 9.5 %copy-start.12 = (bf16[2048,256]{1,0:T(8,128)(2,1)S(1)}, bf16[2048,256]{1,0:T(8,128)(2,1)}, u32[]{:S(2)}) copy-start(bf16[2048,256]{1,0:T(8,128)(2,1)} %all-gather.9.cloned.1.call-done) | copy-start | bytes 3145732
  396.1 13.7 %all-to-all-start.4 = ((f32[8,64,256]{2,1,0:T(8,128)}), f32[8,64,256]{2,1,0:T(8,128)S(1)}, u32[]{:S(2)}, u32[]{:S(2)}) async-start(f32[8,64,256]{2,1,0:T(8,128)} %bitcast.30), calls=%async_computation.4 | async-start | bytes 1048576 | tf_op jit(solution)/shard_map/all_to_all | solution.py:159
Sparse Core Ops, SparseCore 0:
  46.7 31.8 all-gather.10
  80.7 30.9 all-gather.12
  264.0 29.4 all-gather.6
  296.1 28.4 all-gather.8

commit v5 on v3

--- a/solution.py
+++ b/solution.py
@@ -2,7 +2,6 @@
 import jax.numpy as jnp
 from jax import lax
 from jax.sharding import PartitionSpec as P
-
 
 code_range = 127.0
 
@@ -26,11 +25,16 @@
     return arrived.reshape(rows.shape)
 
 
-def shard_partials(left, right, shards):
-    rows, width = left.shape
-    split_left = left.reshape(rows, shards, width // shards)
-    split_right = right.reshape(shards, width // shards, right.shape[-1])
-    partials = jnp.einsum("rkf,kfe->kre", split_left, split_right, preferred_element_type=jnp.float32)
+def ring_gather(value, axis_name):
+    size = lax.axis_size(axis_name)
+    parts = [value]
+    for shift in range(1, size):
+        pairs = [(i, (i + shift) % size) for i in range(size)]
+        parts.append(lax.ppermute(value, axis_name, pairs))
+    return jnp.stack(parts)
+
+
+def sum_partials(partials):
     return jnp.sum(partials.astype(jnp.bfloat16).astype(jnp.float32), axis=0).astype(jnp.bfloat16)
 
 
@@ -57,9 +61,8 @@
     contract_cols = (((1,), (1,)), ((), ()))
     weight_in = w_in[0]
     weight_out = w_out[0]
-    full_in = lax.all_gather(weight_in, "expert", axis=1, tiled=True)
-    full_out = lax.all_gather(weight_out, "expert", axis=0, tiled=True)
-    shards = full_in.shape[1] // weight_in.shape[1]
+    stacked_in = ring_gather(weight_in, "expert")
+    stacked_out = ring_gather(weight_out, "expert")
 
     window = windows[0, 0]
     picked = jnp.take(table[0], window, axis=0).astype(jnp.float32)
@@ -105,10 +108,12 @@
     rows = arrived[:, :width].astype(jnp.bfloat16)
     row_targets = arrived[:, width : width + 3]
     row_live = arrived[:, width + 3 : width + 4]
-    all_rows = lax.all_gather(rows, "expert", axis=0, tiled=True)
-    pre_act = jnp.dot(rows, full_in, preferred_element_type=jnp.float32)
+    all_rows = ring_gather(rows, "expert").reshape(-1, rows.shape[-1])
+    pre_act = jnp.einsum("re,kef->rkf", rows, stacked_in, preferred_element_type=jnp.float32)
     hidden = jax.nn.silu(pre_act).astype(jnp.bfloat16)
-    mixture = shard_partials(hidden, full_out, shards)
+    mixture = sum_partials(
+        jnp.einsum("rkf,kfe->kre", hidden, stacked_out, preferred_element_type=jnp.float32)
+    )
     joined = (rows.astype(jnp.float32) + mixture.astype(jnp.float32)).astype(jnp.bfloat16)
     tower_pre = jnp.einsum("be,kem->kbm", joined, w_tow1, preferred_element_type=jnp.float32)
     logits = jnp.sum(jax.nn.silu(tower_pre) * w_tow2[:, None, :], axis=-1)
@@ -123,12 +128,14 @@
         "kbm,kem->be", tower_grad, w_tow1, preferred_element_type=jnp.float32
     ).astype(jnp.bfloat16)
     row_grads = joined_grad
-    all_grads = lax.all_gather(row_grads, "expert", axis=0, tiled=True)
-    grad_hidden = lax.dot_general(
-        row_grads, full_out, contract_cols, preferred_element_type=jnp.float32
+    all_grads = ring_gather(row_grads, "expert").reshape(-1, row_grads.shape[-1])
+    grad_hidden = jnp.einsum(
+        "re,kfe->rkf", row_grads, stacked_out, preferred_element_type=jnp.float32
     )
     grad_pre = (grad_hidden * silu_slope(pre_act)).astype(jnp.bfloat16)
-    input_grad = shard_partials(grad_pre, full_in.T, shards)
+    input_grad = sum_partials(
+        jnp.einsum("rkf,kef->kre", grad_pre, stacked_in, preferred_element_type=jnp.float32)
+    )
     row_normed_grad = joined_grad.astype(jnp.float32) + input_grad.astype(jnp.float32)
     back = jnp.concatenate(
         [

time: 409 us -> 401 us (0.980)
  the two profiles are of different devices: /device:TPU:8 before, /device:TPU:40 now
where the time goes in v5:
time: 401 us; the launch traced here: 399 us
  waiting for transfers between devices  160 us (40%)
  starting transfers between devices  152 us (38%)
  matrix products  36.5 us (9%)
  local copies, waits for them, and re-layouts  27.2 us (7%)
  other arithmetic  22.3 us (6%)
    ppermute x28, starting transfers between devices, ring_gather(): parts.append(lax.ppermute(value, axis_name, pairs))  78.4 us
    all_to_all x1, waiting for transfers between devices, step(): lax.all_to_all(pooled.reshape(owners, samples, pooled.shape[-1]), 'table'...  74.6 us
    all_to_all x1, waiting for transfers between devices, step(): lax.all_to_all(feature_grad, 'table', split_axis=0, concat_axis=0, tiled=...  57.9 us
    all_to_all x2, starting transfers between devices, to_owners(): lax.all_to_all(shaped, 'table', split_axis=0, concat_axis=0, tiled=True)  28.3 us
    all_to_all x2, waiting for transfers between devices, to_owners(): lax.all_to_all(shaped, 'table', split_axis=0, concat_axis=0, tiled=True)  19.9 us
    all_to_all x1, starting transfers between devices, step(): lax.all_to_all(row_grad.reshape(groups, row_grad.shape[0] // groups, row_...  19.2 us
    all_to_all x1, starting transfers between devices, step(): lax.all_to_all(pooled.reshape(owners, samples, pooled.shape[-1]), 'table'...  16.6 us
    unnamed x60, local copies, waits for them, and re-layouts  16.6 us
  transfers between devices with their start and end apart: 33, of which 7 were waited for; matrix products, arithmetic and copies ran while one was open for 9% of the time, Pallas kernels for 0%

profile of v5, /device:TPU:40, one launch (start us, length us, event | category | flops | bytes accessed | tf_op | source)
XLA Modules:
  0.0 399.3 jit_solution(324673905206338462)
XLA Ops:
  1.8 11.3 %convert_reduce_fusion = bf16[256,8192]{1,0:T(8,128)(2,1)} fusion(s32[8,8192]{1,0:T(8,128)S(1)} %bitcast_select_fusion), kind=kLoop, calls=%fused_computation.4 | loop fusion | flops 48234496 | bytes 4456448 | tf_op jit(solution)/shard_map/reduce_sum | solution.py:19
  16.8 5.5 %convolution_convert_fusion = bf16[8192,256]{1,0:T(8,128)(2,1)} fusion(bf16[256,8192]{1,0:T(8,128)(2,1)} %convert_reduce_fusion, f32[256]{0:T(256)S(1)} %get-tuple-element.36, bf16[256,256]{1,0:T(8,128)(2,1)S(1)} %gather_fusion, pred[256]{0:T(512)(128)(4,1)S(1)} %get-tuple-element.37), kind=kOutput, calls=%fused_computation.6 | convolution fusion | flops 1076166656 | bytes 8520960 | tf_op jit(solution)/shard_map/dot_general | solution.py:72
  22.4 16.6 %all-to-all-start = ((bf16[64,128,256]{2,1,0:T(8,128)(2,1)}), bf16[64,128,256]{2,1,0:T(8,128)(2,1)}, u32[]{:S(2)}, u32[]{:S(2)}) async-start(bf16[64,128,256]{2,1,0:T(8,128)(2,1)} %bitcast.144), calls=%async_computation | async-start | bytes 8388608 | tf_op jit(solution)/shard_map/all_to_all | solution.py:75
  39.0 3.4 collective-permute-start.1
  42.4 4.0 %collective-permute-start.2 = (bf16[256,512]{1,0:T(8,128)(2,1)S(1)}, bf16[256,512]{1,0:T(8,128)(2,1)}, u32[]{:S(2)}, u32[]{:S(2)}) collective-permute-start(bf16[256,512]{1,0:T(8,128)(2,1)S(1)} %bitcast.150), channel_id=1, source_target_pairs={{0,3},{1,4},{2,5},{3,6},{4,7},{5,0},{6,1},{7,2},{8,11},{9,12},{10,... | collective-permute-start | bytes 786440 | tf_op jit(solution)/shard_map/ppermute | solution.py:33
  46.4 3.9 collective-permute-start.3
  50.4 3.5 collective-permute-start.4
  55.1 3.3 collective-permute-start.5
  69.3 5.9 %collective-permute-start.10 = (bf16[512,256]{1,0:T(8,128)(2,1)S(1)}, bf16[512,256]{1,0:T(8,128)(2,1)S(1)}, u32[]{:S(2)}, u32[]{:S(2)}) collective-permute-start(bf16[512,256]{1,0:T(8,128)(2,1)S(1)} %bitcast.159), channel_id=1, source_target_pairs={{0,4},{1,5},{2,6},{3,7},{4,0},{5,1},{6,2},{7,3},{8,12},{9,13},{10,... | collective-permute-start | bytes 786440 | tf_op jit(solution)/shard_map/ppermute | solution.py:33
  75.2 2.8 collective-permute-start.11
  78.1 3.2 collective-permute-start.12
  85.1 74.6 %all-to-all-done = bf16[64,128,256]{2,1,0:T(8,128)(2,1)} async-done(((bf16[64,128,256]{2,1,0:T(8,128)(2,1)}), bf16[64,128,256]{2,1,0:T(8,128)(2,1)}, u32[]{:S(2)}, u32[]{:S(2)}) %all-to-all-start) | async-done | bytes 4194336 | tf_op jit(solution)/shard_map/all_to_all | solution.py:75
  159.7 3.1 multiply_reduce_fusion
  165.1 20.0 %all-to-all-start.1 = ((f32[64,4,384]{2,1,0:T(4,128)}), f32[64,4,384]{2,1,0:T(4,128)S(1)}, u32[]{:S(2)}, u32[]{:S(2)}) async-start(f32[64,4,384]{2,1,0:T(4,128)} %broadcast_select_fusion), calls=%async_computation.1 | async-start | bytes 786432 | tf_op jit(solution)/shard_map/all_to_all | solution.py:24
  190.9 6.9 %all-to-all-done.1 = f32[64,4,384]{2,1,0:T(4,128)S(1)} async-done(((f32[64,4,384]{2,1,0:T(4,128)}), f32[64,4,384]{2,1,0:T(4,128)S(1)}, u32[]{:S(2)}, u32[]{:S(2)}) %all-to-all-start.1) | async-done | bytes 393248 | tf_op jit(solution)/shard_map/all_to_all | solution.py:24
  207.6 5.3 %fusion.7 = bf16[256,256]{1,0:T(8,128)(2,1)S(1)} fusion(bf16[8,256,512]{2,1,0:T(8,128)(2,1)} %copy-done.4, f32[256,8,512]{2,0,1:T(8,128)} %copy-done.2, bf16[8,512,256]{2,1,0:T(8,128)(2,1)} %bitcast_dynamic-update-slice_fusion, bf16[256,256]{1,0:T(8,128)(2,1)S(1)} %get-tuple-element.47), kind=kOutput, calls=%fused_computation.24 | convolution fusion | flops 1084162048 | bytes 8650752 | tf_op jit(solution)/shard_map/rkf,kef->kre/dot_general | solution.py:137
  215.0 8.3 %all-to-all-start.2 = ((f32[64,4,384]{2,1,0:T(4,128)}), f32[64,4,384]{2,1,0:T(4,128)S(1)}, u32[]{:S(2)}, u32[]{:S(2)}) async-start(f32[64,4,384]{2,1,0:T(4,128)} %concatenate.19), calls=%async_computation.2 | async-start | bytes 786432 | tf_op jit(solution)/shard_map/all_to_all | solution.py:24
  223.3 13.0 %all-to-all-done.2 = f32[64,4,384]{2,1,0:T(4,128)S(1)} async-done(((f32[64,4,384]{2,1,0:T(4,128)}), f32[64,4,384]{2,1,0:T(4,128)S(1)}, u32[]{:S(2)}, u32[]{:S(2)}) %all-to-all-start.2) | async-done | bytes 393248 | tf_op jit(solution)/shard_map/all_to_all | solution.py:24
  237.5 3.4 multiply_convert_fusion
  240.9 9.1 %all-to-all-start.3 = ((bf16[64,128,256]{2,1,0:T(8,128)(2,1)}), bf16[64,128,256]{2,1,0:T(8,128)(2,1)}, u32[]{:S(2)}, u32[]{:S(2)}) async-start(bf16[64,128,256]{2,1,0:T(8,128)(2,1)} %multiply_convert_fusion), calls=%async_computation.3 | async-start | bytes 8388608 | tf_op jit(solution)/shard_map/all_to_all | solution.py:157
  250.0 7.2 %collective-permute-start.15 = (bf16[256,256]{1,0:T(8,128)(2,1)S(1)}, bf16[256,256]{1,0:T(8,128)(2,1)S(1)}, u32[]{:S(2)}, u32[]{:S(2)}) collective-permute-start(bf16[256,256]{1,0:T(8,128)(2,1)S(1)} %get-tuple-element.29), channel_id=1, source_target_pairs={{0,2},{1,3},{2,4},{3,5},{4,6},{5,7},{6,0},{7,1},{8,10},{9,11},{10,... | collective-permute-start | bytes 393224 | tf_op jit(solution)/shard_map/ppermute | solution.py:33
  257.3 6.7 %collective-permute-start.16 = (bf16[256,256]{1,0:T(8,128)(2,1)S(1)}, bf16[256,256]{1,0:T(8,128)(2,1)S(1)}, u32[]{:S(2)}, u32[]{:S(2)}) collective-permute-start(bf16[256,256]{1,0:T(8,128)(2,1)S(1)} %get-tuple-element.29), channel_id=1, source_target_pairs={{0,3},{1,4},{2,5},{3,6},{4,7},{5,0},{6,1},{7,2},{8,11},{9,12},{10,... | collective-permute-start | bytes 393224 | tf_op jit(solution)/shard_map/ppermute | solution.py:33
  266.5 4.9 %collective-permute-start.18 = (bf16[256,256]{1,0:T(8,128)(2,1)S(1)}, bf16[256,256]{1,0:T(8,128)(2,1)S(1)}, u32[]{:S(2)}, u32[]{:S(2)}) collective-permute-start(bf16[256,256]{1,0:T(8,128)(2,1)S(1)} %get-tuple-element.29), channel_id=1, source_target_pairs={{0,5},{1,6},{2,7},{3,0},{4,1},{5,2},{6,3},{7,4},{8,13},{9,14},{10,... | collective-permute-start | bytes 393224 | tf_op jit(solution)/shard_map/ppermute | solution.py:33
  273.9 3.9 collective-permute-start.22
  279.9 5.5 %collective-permute-start.24 = (bf16[256,256]{1,0:T(8,128)(2,1)S(1)}, bf16[256,256]{1,0:T(8,128)(2,1)S(1)}, u32[]{:S(2)}, u32[]{:S(2)}) collective-permute-start(bf16[256,256]{1,0:T(8,128)(2,1)S(1)} %get-tuple-element.47), channel_id=1, source_target_pairs={{0,4},{1,5},{2,6},{3,7},{4,0},{5,1},{6,2},{7,3},{8,12},{9,13},{10,... | collective-permute-start | bytes 393224 | tf_op jit(solution)/shard_map/ppermute | solution.py:33
  287.4 4.5 %collective-permute-start.26 = (bf16[256,256]{1,0:T(8,128)(2,1)S(1)}, bf16[256,256]{1,0:T(8,128)(2,1)S(1)}, u32[]{:S(2)}, u32[]{:S(2)}) collective-permute-start(bf16[256,256]{1,0:T(8,128)(2,1)S(1)} %get-tuple-element.47), channel_id=1, source_target_pairs={{0,6},{1,7},{2,0},{3,1},{4,2},{5,3},{6,4},{7,5},{8,14},{9,15},{10,... | collective-permute-start | bytes 393224 | tf_op jit(solution)/shard_map/ppermute | solution.py:33
  299.8 5.4 %fusion.8 = f32[1,256,512]{2,1,0:T(8,128)} fusion(bf16[2048,256]{1,0:T(8,128)(2,1)S(1)} %bitcast.147, f32[2048,512]{1,0:T(8,128)} %fusion.38, bf16[2048,256]{1,0:T(8,128)(2,1)} %bitcast.174, bf16[1,512,256]{2,1,0:T(8,128)(2,1)S(1)} %copy-done.7), kind=kOutput, calls=%fused_computation.25 | convolution fusion | flops 1083179008 | bytes 7077888 | tf_op jit(solution)/shard_map/dot_general | solution.py:184
  305.2 57.9 %all-to-all-done.3 = bf16[64,128,256]{2,1,0:T(8,128)(2,1)} async-done(((bf16[64,128,256]{2,1,0:T(8,128)(2,1)}), bf16[64,128,256]{2,1,0:T(8,128)(2,1)}, u32[]{:S(2)}, u32[]{:S(2)}) %all-to-all-start.3) | async-done | bytes 4194336 | tf_op jit(solution)/shard_map/all_to_all | solution.py:157
  363.1 4.8 %fusion.51 = f32[256,256]{1,0:T(8,128)S(1)} fusion(bf16[256,8192]{1,0:T(8,128)(2,1)} %convert_reduce_fusion, bf16[8192,256]{1,0:T(8,128)(2,1)} %bitcast.42), kind=kOutput, calls=%fused_computation.143 | convolution fusion | flops 1073741824 | bytes 8650752 | tf_op jit(solution)/shard_map/dot_general | solution.py:160
  369.1 19.2 %all-to-all-start.4 = ((f32[8,64,256]{2,1,0:T(8,128)}), f32[8,64,256]{2,1,0:T(8,128)S(1)}, u32[]{:S(2)}, u32[]{:S(2)}) async-start(f32[8,64,256]{2,1,0:T(8,128)} %bitcast.43), calls=%async_computation.4 | async-start | bytes 1048576 | tf_op jit(solution)/shard_map/all_to_all | solution.py:166
  388.4 4.3 %fusion.9 = f32[1,512,256]{2,1,0:T(8,128)} fusion(bf16[2048,256]{1,0:T(8,128)(2,1)S(1)} %bitcast.175, f32[2048,512]{1,0:T(8,128)} %fusion.38), kind=kOutput, calls=%fused_computation.26 | convolution fusion | flops 542113792 | bytes 5767168 | tf_op jit(solution)/shard_map/dot_general | solution.py:181
  393.3 5.4 %all-to-all-done.4 = f32[8,64,256]{2,1,0:T(8,128)S(1)} async-done(((f32[8,64,256]{2,1,0:T(8,128)}), f32[8,64,256]{2,1,0:T(8,128)S(1)}, u32[]{:S(2)}, u32[]{:S(2)}) %all-to-all-start.4) | async-done | bytes 524320 | tf_op jit(solution)/shard_map/all_to_all | solution.py:166
  (161 shorter events, 61.1 us)
Async XLA Ops:
  22.4 137.3 %all-to-all-start = ((bf16[64,128,256]{2,1,0:T(8,128)(2,1)}), bf16[64,128,256]{2,1,0:T(8,128)(2,1)}, u32[]{:S(2)}, u32[]{:S(2)}) async-start(bf16[64,128,256]{2,1,0:T(8,128)(2,1)} %bitcast.144), calls=%async_computation | async-start | bytes 8388608 | tf_op jit(solution)/shard_map/all_to_all | solution.py:75
  39.0 16.1 %collective-permute-start = (bf16[256,512]{1,0:T(8,128)(2,1)S(1)}, bf16[256,512]{1,0:T(8,128)(2,1)}, u32[]{:S(2)}, u32[]{:S(2)}) collective-permute-start(bf16[256,512]{1,0:T(8,128)(2,1)S(1)} %bitcast.148), channel_id=1, source_target_pairs={{0,1},{1,2},{2,3},{3,4},{4,5},{5,6},{6,7},{7,0},{8,9},{9,10},{10,1... | collective-permute-start | bytes 786440 | tf_op jit(solution)/shard_map/ppermute | solution.py:33
  39.0 20.3 %collective-permute-start.1 = (bf16[256,512]{1,0:T(8,128)(2,1)S(1)}, bf16[256,512]{1,0:T(8,128)(2,1)}, u32[]{:S(2)}, u32[]{:S(2)}) collective-permute-start(bf16[256,512]{1,0:T(8,128)(2,1)S(1)} %bitcast.149), channel_id=1, source_target_pairs={{0,2},{1,3},{2,4},{3,5},{4,6},{5,7},{6,0},{7,1},{8,10},{9,11},{10,... | collective-permute-start | bytes 786440 | tf_op jit(solution)/shard_map/ppermute | solution.py:33
  42.4 17.9 %collective-permute-start.2 = (bf16[256,512]{1,0:T(8,128)(2,1)S(1)}, bf16[256,512]{1,0:T(8,128)(2,1)}, u32[]{:S(2)}, u32[]{:S(2)}) collective-permute-start(bf16[256,512]{1,0:T(8,128)(2,1)S(1)} %bitcast.150), channel_id=1, source_target_pairs={{0,3},{1,4},{2,5},{3,6},{4,7},{5,0},{6,1},{7,2},{8,11},{9,12},{10,... | collective-permute-start | bytes 786440 | tf_op jit(solution)/shard_map/ppermute | solution.py:33
  46.4 17.2 %collective-permute-start.3 = (bf16[256,512]{1,0:T(8,128)(2,1)S(1)}, bf16[256,512]{1,0:T(8,128)(2,1)}, u32[]{:S(2)}, u32[]{:S(2)}) collective-permute-start(bf16[256,512]{1,0:T(8,128)(2,1)S(1)} %bitcast.151), channel_id=1, source_target_pairs={{0,4},{1,5},{2,6},{3,7},{4,0},{5,1},{6,2},{7,3},{8,12},{9,13},{10,... | collective-permute-start | bytes 786440 | tf_op jit(solution)/shard_map/ppermute | solution.py:33
  50.4 16.1 %collective-permute-start.4 = (bf16[256,512]{1,0:T(8,128)(2,1)S(1)}, bf16[256,512]{1,0:T(8,128)(2,1)S(1)}, u32[]{:S(2)}, u32[]{:S(2)}) collective-permute-start(bf16[256,512]{1,0:T(8,128)(2,1)S(1)} %bitcast.152), channel_id=1, source_target_pairs={{0,5},{1,6},{2,7},{3,0},{4,1},{5,2},{6,3},{7,4},{8,13},{9,14},{10,... | collective-permute-start | bytes 786440 | tf_op jit(solution)/shard_map/ppermute | solution.py:33
  55.1 14.3 %collective-permute-start.5 = (bf16[256,512]{1,0:T(8,128)(2,1)S(1)}, bf16[256,512]{1,0:T(8,128)(2,1)S(1)}, u32[]{:S(2)}, u32[]{:S(2)}) collective-permute-start(bf16[256,512]{1,0:T(8,128)(2,1)S(1)} %bitcast.153), channel_id=1, source_target_pairs={{0,6},{1,7},{2,0},{3,1},{4,2},{5,3},{6,4},{7,5},{8,14},{9,15},{10,... | collective-permute-start | bytes 786440 | tf_op jit(solution)/shard_map/ppermute | solution.py:33
  59.4 15.8 %collective-permute-start.6 = (bf16[256,512]{1,0:T(8,128)(2,1)S(1)}, bf16[256,512]{1,0:T(8,128)(2,1)S(1)}, u32[]{:S(2)}, u32[]{:S(2)}) collective-permute-start(bf16[256,512]{1,0:T(8,128)(2,1)S(1)} %bitcast.154), channel_id=1, source_target_pairs={{0,7},{1,0},{2,1},{3,2},{4,3},{5,4},{6,5},{7,6},{8,15},{9,8},{10,9... | collective-permute-start | bytes 786440 | tf_op jit(solution)/shard_map/ppermute | solution.py:33
  60.4 17.7 %collective-permute-start.7 = (bf16[512,256]{1,0:T(8,128)(2,1)S(1)}, bf16[512,256]{1,0:T(8,128)(2,1)S(1)}, u32[]{:S(2)}, u32[]{:S(2)}) collective-permute-start(bf16[512,256]{1,0:T(8,128)(2,1)S(1)} %bitcast.156), channel_id=1, source_target_pairs={{0,1},{1,2},{2,3},{3,4},{4,5},{5,6},{6,7},{7,0},{8,9},{9,10},{10,1... | collective-permute-start | bytes 786440 | tf_op jit(solution)/shard_map/ppermute | solution.py:33
  63.6 18.4 %collective-permute-start.8 = (bf16[512,256]{1,0:T(8,128)(2,1)S(1)}, bf16[512,256]{1,0:T(8,128)(2,1)S(1)}, u32[]{:S(2)}, u32[]{:S(2)}) collective-permute-start(bf16[512,256]{1,0:T(8,128)(2,1)S(1)} %bitcast.157), channel_id=1, source_target_pairs={{0,2},{1,3},{2,4},{3,5},{4,6},{5,7},{6,0},{7,1},{8,10},{9,11},{10,... | collective-permute-start | bytes 786440 | tf_op jit(solution)/shard_map/ppermute | solution.py:33
  66.5 17.8 %collective-permute-start.9 = (bf16[512,256]{1,0:T(8,128)(2,1)S(1)}, bf16[512,256]{1,0:T(8,128)(2,1)S(1)}, u32[]{:S(2)}, u32[]{:S(2)}) collective-permute-start(bf16[512,256]{1,0:T(8,128)(2,1)S(1)} %bitcast.158), channel_id=1, source_target_pairs={{0,3},{1,4},{2,5},{3,6},{4,7},{5,0},{6,1},{7,2},{8,11},{9,12},{10,... | collective-permute-start | bytes 786440 | tf_op jit(solution)/shard_map/ppermute | solution.py:33
  69.3 115.8 %collective-permute-start.10 = (bf16[512,256]{1,0:T(8,128)(2,1)S(1)}, bf16[512,256]{1,0:T(8,128)(2,1)S(1)}, u32[]{:S(2)}, u32[]{:S(2)}) collective-permute-start(bf16[512,256]{1,0:T(8,128)(2,1)S(1)} %bitcast.159), channel_id=1, source_target_pairs={{0,4},{1,5},{2,6},{3,7},{4,0},{5,1},{6,2},{7,3},{8,12},{9,13},{10,... | collective-permute-start | bytes 786440 | tf_op jit(solution)/shard_map/ppermute | solution.py:33
  75.2 110.7 %collective-permute-start.11 = (bf16[512,256]{1,0:T(8,128)(2,1)S(1)}, bf16[512,256]{1,0:T(8,128)(2,1)}, u32[]{:S(2)}, u32[]{:S(2)}) collective-permute-start(bf16[512,256]{1,0:T(8,128)(2,1)S(1)} %bitcast.160), channel_id=1, source_target_pairs={{0,5},{1,6},{2,7},{3,0},{4,1},{5,2},{6,3},{7,4},{8,13},{9,14},{10,... | collective-permute-start | bytes 786440 | tf_op jit(solution)/shard_map/ppermute | solution.py:33
  78.1 109.5 %collective-permute-start.12 = (bf16[512,256]{1,0:T(8,128)(2,1)S(1)}, bf16[512,256]{1,0:T(8,128)(2,1)}, u32[]{:S(2)}, u32[]{:S(2)}) collective-permute-start(bf16[512,256]{1,0:T(8,128)(2,1)S(1)} %bitcast.161), channel_id=1, source_target_pairs={{0,6},{1,7},{2,0},{3,1},{4,2},{5,3},{6,4},{7,5},{8,14},{9,15},{10,... | collective-permute-start | bytes 786440 | tf_op jit(solution)/shard_map/ppermute | solution.py:33
  82.0 107.2 %collective-permute-start.13 = (bf16[512,256]{1,0:T(8,128)(2,1)S(1)}, bf16[512,256]{1,0:T(8,128)(2,1)}, u32[]{:S(2)}, u32[]{:S(2)}) collective-permute-start(bf16[512,256]{1,0:T(8,128)(2,1)S(1)} %bitcast.162), channel_id=1, source_target_pairs={{0,7},{1,0},{2,1},{3,2},{4,3},{5,4},{6,5},{7,6},{8,15},{9,8},{10,9... | collective-permute-start | bytes 786440 | tf_op jit(solution)/shard_map/ppermute | solution.py:33
  165.1 32.7 %all-to-all-start.1 = ((f32[64,4,384]{2,1,0:T(4,128)}), f32[64,4,384]{2,1,0:T(4,128)S(1)}, u32[]{:S(2)}, u32[]{:S(2)}) async-start(f32[64,4,384]{2,1,0:T(4,128)} %broadcast_select_fusion), calls=%async_computation.1 | async-start | bytes 786432 | tf_op jit(solution)/shard_map/all_to_all | solution.py:24
  215.0 21.3 %all-to-all-start.2 = ((f32[64,4,384]{2,1,0:T(4,128)}), f32[64,4,384]{2,1,0:T(4,128)S(1)}, u32[]{:S(2)}, u32[]{:S(2)}) async-start(f32[64,4,384]{2,1,0:T(4,128)} %concatenate.19), calls=%async_computation.2 | async-start | bytes 786432 | tf_op jit(solution)/shard_map/all_to_all | solution.py:24
  240.9 122.2 %all-to-all-start.3 = ((bf16[64,128,256]{2,1,0:T(8,128)(2,1)}), bf16[64,128,256]{2,1,0:T(8,128)(2,1)}, u32[]{:S(2)}, u32[]{:S(2)}) async-start(bf16[64,128,256]{2,1,0:T(8,128)(2,1)} %multiply_convert_fusion), calls=%async_computation.3 | async-start | bytes 8388608 | tf_op jit(solution)/shard_map/all_to_all | solution.py:157
  250.0 21.4 %collective-permute-start.14 = (bf16[256,256]{1,0:T(8,128)(2,1)S(1)}, bf16[256,256]{1,0:T(8,128)(2,1)S(1)}, u32[]{:S(2)}, u32[]{:S(2)}) collective-permute-start(bf16[256,256]{1,0:T(8,128)(2,1)S(1)} %get-tuple-element.29), channel_id=1, source_target_pairs={{0,1},{1,2},{2,3},{3,4},{4,5},{5,6},{6,7},{7,0},{8,9},{9,10},{10,1... | collective-permute-start | bytes 393224 | tf_op jit(solution)/shard_map/ppermute | solution.py:33
  250.0 23.3 %collective-permute-start.15 = (bf16[256,256]{1,0:T(8,128)(2,1)S(1)}, bf16[256,256]{1,0:T(8,128)(2,1)S(1)}, u32[]{:S(2)}, u32[]{:S(2)}) collective-permute-start(bf16[256,256]{1,0:T(8,128)(2,1)S(1)} %get-tuple-element.29), channel_id=1, source_target_pairs={{0,2},{1,3},{2,4},{3,5},{4,6},{5,7},{6,0},{7,1},{8,10},{9,11},{10,... | collective-permute-start | bytes 393224 | tf_op jit(solution)/shard_map/ppermute | solution.py:33
  257.3 16.4 %collective-permute-start.16 = (bf16[256,256]{1,0:T(8,128)(2,1)S(1)}, bf16[256,256]{1,0:T(8,128)(2,1)S(1)}, u32[]{:S(2)}, u32[]{:S(2)}) collective-permute-start(bf16[256,256]{1,0:T(8,128)(2,1)S(1)} %get-tuple-element.29), channel_id=1, source_target_pairs={{0,3},{1,4},{2,5},{3,6},{4,7},{5,0},{6,1},{7,2},{8,11},{9,12},{10,... | collective-permute-start | bytes 393224 | tf_op jit(solution)/shard_map/ppermute | solution.py:33
  264.0 10.0 %collective-permute-start.17 = (bf16[256,256]{1,0:T(8,128)(2,1)S(1)}, bf16[256,256]{1,0:T(8,128)(2,1)S(1)}, u32[]{:S(2)}, u32[]{:S(2)}) collective-permute-start(bf16[256,256]{1,0:T(8,128)(2,1)S(1)} %get-tuple-element.29), channel_id=1, source_target_pairs={{0,4},{1,5},{2,6},{3,7},{4,0},{5,1},{6,2},{7,3},{8,12},{9,13},{10,... | collective-permute-start | bytes 393224 | tf_op jit(solution)/shard_map/ppermute | solution.py:33
  266.5 11.4 %collective-permute-start.18 = (bf16[256,256]{1,0:T(8,128)(2,1)S(1)}, bf16[256,256]{1,0:T(8,128)(2,1)S(1)}, u32[]{:S(2)}, u32[]{:S(2)}) collective-permute-start(bf16[256,256]{1,0:T(8,128)(2,1)S(1)} %get-tuple-element.29), channel_id=1, source_target_pairs={{0,5},{1,6},{2,7},{3,0},{4,1},{5,2},{6,3},{7,4},{8,13},{9,14},{10,... | collective-permute-start | bytes 393224 | tf_op jit(solution)/shard_map/ppermute | solution.py:33
  271.4 8.5 %collective-permute-start.19 = (bf16[256,256]{1,0:T(8,128)(2,1)S(1)}, bf16[256,256]{1,0:T(8,128)(2,1)S(1)}, u32[]{:S(2)}, u32[]{:S(2)}) collective-permute-start(bf16[256,256]{1,0:T(8,128)(2,1)S(1)} %get-tuple-element.29), channel_id=1, source_target_pairs={{0,6},{1,7},{2,0},{3,1},{4,2},{5,3},{6,4},{7,5},{8,14},{9,15},{10,... | collective-permute-start | bytes 393224 | tf_op jit(solution)/shard_map/ppermute | solution.py:33
  273.4 12.1 %collective-permute-start.20 = (bf16[256,256]{1,0:T(8,128)(2,1)S(1)}, bf16[256,256]{1,0:T(8,128)(2,1)S(1)}, u32[]{:S(2)}, u32[]{:S(2)}) collective-permute-start(bf16[256,256]{1,0:T(8,128)(2,1)S(1)} %get-tuple-element.29), channel_id=1, source_target_pairs={{0,7},{1,0},{2,1},{3,2},{4,3},{5,4},{6,5},{7,6},{8,15},{9,8},{10,9... | collective-permute-start | bytes 393224 | tf_op jit(solution)/shard_map/ppermute | solution.py:33
  273.7 13.7 %collective-permute-start.21 = (bf16[256,256]{1,0:T(8,128)(2,1)S(1)}, bf16[256,256]{1,0:T(8,128)(2,1)S(1)}, u32[]{:S(2)}, u32[]{:S(2)}) collective-permute-start(bf16[256,256]{1,0:T(8,128)(2,1)S(1)} %get-tuple-element.47), channel_id=1, source_target_pairs={{0,1},{1,2},{2,3},{3,4},{4,5},{5,6},{6,7},{7,0},{8,9},{9,10},{10,1... | collective-permute-start | bytes 393224 | tf_op jit(solution)/shard_map/ppermute | solution.py:33
  273.9 18.6 %collective-permute-start.22 = (bf16[256,256]{1,0:T(8,128)(2,1)S(1)}, bf16[256,256]{1,0:T(8,128)(2,1)S(1)}, u32[]{:S(2)}, u32[]{:S(2)}) collective-permute-start(bf16[256,256]{1,0:T(8,128)(2,1)S(1)} %get-tuple-element.47), channel_id=1, source_target_pairs={{0,2},{1,3},{2,4},{3,5},{4,6},{5,7},{6,0},{7,1},{8,10},{9,11},{10,... | collective-permute-start | bytes 393224 | tf_op jit(solution)/shard_map/ppermute | solution.py:33
  277.9 15.3 %collective-permute-start.23 = (bf16[256,256]{1,0:T(8,128)(2,1)S(1)}, bf16[256,256]{1,0:T(8,128)(2,1)S(1)}, u32[]{:S(2)}, u32[]{:S(2)}) collective-permute-start(bf16[256,256]{1,0:T(8,128)(2,1)S(1)} %get-tuple-element.47), channel_id=1, source_target_pairs={{0,3},{1,4},{2,5},{3,6},{4,7},{5,0},{6,1},{7,2},{8,11},{9,12},{10,... | collective-permute-start | bytes 393224 | tf_op jit(solution)/shard_map/ppermute | solution.py:33
  279.9 13.9 %collective-permute-start.24 = (bf16[256,256]{1,0:T(8,128)(2,1)S(1)}, bf16[256,256]{1,0:T(8,128)(2,1)S(1)}, u32[]{:S(2)}, u32[]{:S(2)}) collective-permute-start(bf16[256,256]{1,0:T(8,128)(2,1)S(1)} %get-tuple-element.47), channel_id=1, source_target_pairs={{0,4},{1,5},{2,6},{3,7},{4,0},{5,1},{6,2},{7,3},{8,12},{9,13},{10,... | collective-permute-start | bytes 393224 | tf_op jit(solution)/shard_map/ppermute | solution.py:33
  285.4 9.1 %collective-permute-start.25 = (bf16[256,256]{1,0:T(8,128)(2,1)S(1)}, bf16[256,256]{1,0:T(8,128)(2,1)S(1)}, u32[]{:S(2)}, u32[]{:S(2)}) collective-permute-start(bf16[256,256]{1,0:T(8,128)(2,1)S(1)} %get-tuple-element.47), channel_id=1, source_target_pairs={{0,5},{1,6},{2,7},{3,0},{4,1},{5,2},{6,3},{7,4},{8,13},{9,14},{10,... | collective-permute-start | bytes 393224 | tf_op jit(solution)/shard_map/ppermute | solution.py:33
  287.4 8.4 %collective-permute-start.26 = (bf16[256,256]{1,0:T(8,128)(2,1)S(1)}, bf16[256,256]{1,0:T(8,128)(2,1)S(1)}, u32[]{:S(2)}, u32[]{:S(2)}) collective-permute-start(bf16[256,256]{1,0:T(8,128)(2,1)S(1)} %get-tuple-element.47), channel_id=1, source_target_pairs={{0,6},{1,7},{2,0},{3,1},{4,2},{5,3},{6,4},{7,5},{8,14},{9,15},{10,... | collective-permute-start | bytes 393224 | tf_op jit(solution)/shard_map/ppermute | solution.py:33
  369.1 29.5 %all-to-all-start.4 = ((f32[8,64,256]{2,1,0:T(8,128)}), f32[8,64,256]{2,1,0:T(8,128)S(1)}, u32[]{:S(2)}, u32[]{:S(2)}) async-start(f32[8,64,256]{2,1,0:T(8,128)} %bitcast.43), calls=%async_computation.4 | async-start | bytes 1048576 | tf_op jit(solution)/shard_map/all_to_all | solution.py:166
  (16 other events, 600.6 us)

commit v6 on v5

--- a/solution.py
+++ b/solution.py
@@ -94,20 +94,21 @@
     source = jnp.sum(placing * jnp.arange(1, samples + 1, dtype=jnp.int32)[None, :], axis=1)
     width = normed.shape[-1]
     lanes = 128 * (-(-(width + 4) // 128))
-    payload = jnp.concatenate(
+    extra = 128
+    labels = jnp.concatenate(
         [
-            normed.astype(jnp.float32),
             targets[0],
             jnp.ones((samples, 1), jnp.float32),
-            jnp.zeros((samples, lanes - width - 4), jnp.float32),
+            jnp.zeros((samples, extra - 4), jnp.float32),
         ],
         axis=1,
     )
-    padded = jnp.concatenate([jnp.zeros((1, lanes), jnp.float32), payload], axis=0)
-    arrived = to_owners(jnp.take(padded, source, axis=0), owners)
-    rows = arrived[:, :width].astype(jnp.bfloat16)
-    row_targets = arrived[:, width : width + 3]
-    row_live = arrived[:, width + 3 : width + 4]
+    padded_labels = jnp.concatenate([jnp.zeros((1, extra), jnp.float32), labels], axis=0)
+    row_labels = to_owners(jnp.take(padded_labels, source, axis=0), owners)
+    row_targets = row_labels[:, :3]
+    row_live = row_labels[:, 3:4]
+    padded = jnp.concatenate([jnp.zeros((1, width), normed.dtype), normed], axis=0)
+    rows = to_owners(jnp.take(padded, source, axis=0), owners)
     all_rows = ring_gather(rows, "expert").reshape(-1, rows.shape[-1])
     pre_act = jnp.einsum("re,kef->rkf", rows, stacked_in, preferred_element_type=jnp.float32)
     hidden = jax.nn.silu(pre_act).astype(jnp.bfloat16)

time: 401 us -> 411 us (1.025)
  the two profiles are of different devices: /device:TPU:40 before, /device:TPU:32 now
where the time goes in v6:
time: 411 us; the launch traced here: 410 us
  waiting for transfers between devices  161 us (39%)
  starting transfers between devices  156 us (38%)
  matrix products  34.4 us (8%)
  local copies, waits for them, and re-layouts  30 us (7%)
  other arithmetic  26.5 us (6%)
    ppermute x28, starting transfers between devices, ring_gather(): parts.append(lax.ppermute(value, axis_name, pairs))  73.6 us
    all_to_all x1, waiting for transfers between devices, step(): lax.all_to_all(pooled.reshape(owners, samples, pooled.shape[-1]), 'table'...  70.2 us
    all_to_all x1, waiting for transfers between devices, step(): lax.all_to_all(feature_grad, 'table', split_axis=0, concat_axis=0, tiled=...  65 us
    all_to_all x3, starting transfers between devices, to_owners(): lax.all_to_all(shaped, 'table', split_axis=0, concat_axis=0, tiled=True)  46.4 us
    unnamed x62, local copies, waits for them, and re-layouts  18.5 us
    all_to_all x3, waiting for transfers between devices, to_owners(): lax.all_to_all(shaped, 'table', split_axis=0, concat_axis=0, tiled=True)  16.6 us
    all_to_all x1, starting transfers between devices, step(): lax.all_to_all(row_grad.reshape(groups, row_grad.shape[0] // groups, row_...  13.5 us
    all_to_all x1, starting transfers between devices, step(): lax.all_to_all(pooled.reshape(owners, samples, pooled.shape[-1]), 'table'...  13 us
  transfers between devices with their start and end apart: 34, of which 9 were waited for; matrix products, arithmetic and copies ran while one was open for 14% of the time, Pallas kernels for 0%

profile of v6, /device:TPU:32, one launch (start us, length us, event | category | flops | bytes accessed | tf_op | source)
XLA Modules:
  0.0 409.5 jit_solution(1973968525743423839)
XLA Ops:
  6.6 16.3 %all-to-all-start.2 = ((f32[64,4,128]{2,1,0:T(4,128)}), f32[64,4,128]{2,1,0:T(4,128)S(1)}, u32[]{:S(2)}, u32[]{:S(2)}) async-start(f32[64,4,128]{2,1,0:T(4,128)} %broadcast_select_fusion.2), calls=%async_computation.2 | async-start | bytes 262144 | tf_op jit(solution)/shard_map/all_to_all | solution.py:24
  24.0 11.3 %convert_reduce_fusion = bf16[256,8192]{1,0:T(8,128)(2,1)} fusion(s32[8,8192]{1,0:T(8,128)S(1)} %bitcast_select_fusion), kind=kLoop, calls=%fused_computation.5 | loop fusion | flops 48234496 | bytes 4456448 | tf_op jit(solution)/shard_map/reduce_sum | solution.py:19
  38.4 5.6 %convolution_convert_fusion = bf16[8192,256]{1,0:T(8,128)(2,1)} fusion(bf16[256,8192]{1,0:T(8,128)(2,1)} %convert_reduce_fusion, f32[256]{0:T(256)S(1)} %get-tuple-element.26, bf16[256,256]{1,0:T(8,128)(2,1)S(1)} %gather_fusion, pred[256]{0:T(512)(128)(4,1)S(1)} %get-tuple-element.27), kind=kOutput, calls=%fused_computation.7 | convolution fusion | flops 1076166656 | bytes 8520960 | tf_op jit(solution)/shard_map/dot_general | solution.py:72
  43.9 13.0 %all-to-all-start = ((bf16[64,128,256]{2,1,0:T(8,128)(2,1)}), bf16[64,128,256]{2,1,0:T(8,128)(2,1)}, u32[]{:S(2)}, u32[]{:S(2)}) async-start(bf16[64,128,256]{2,1,0:T(8,128)(2,1)} %bitcast.143), calls=%async_computation | async-start | bytes 8388608 | tf_op jit(solution)/shard_map/all_to_all | solution.py:75
  57.0 3.4 collective-permute-start.1
  60.4 4.0 collective-permute-start.2
  64.4 3.9 collective-permute-start.3
  68.4 3.5 collective-permute-start.4
  73.9 3.4 collective-permute-start.5
  87.3 5.8 %collective-permute-start.10 = (bf16[512,256]{1,0:T(8,128)(2,1)}, bf16[512,256]{1,0:T(8,128)(2,1)S(1)}, u32[]{:S(2)}, u32[]{:S(2)}) collective-permute-start(bf16[512,256]{1,0:T(8,128)(2,1)} %bitcast.20), channel_id=1, source_target_pairs={{0,4},{1,5},{2,6},{3,7},{4,0},{5,1},{6,2},{7,3},{8,12},{9,13},{10,... | collective-permute-start | bytes 786440 | tf_op jit(solution)/shard_map/ppermute | solution.py:33
  95.4 3.5 collective-permute-start.12
  105.7 70.2 %all-to-all-done = bf16[64,128,256]{2,1,0:T(8,128)(2,1)} async-done(((bf16[64,128,256]{2,1,0:T(8,128)(2,1)}), bf16[64,128,256]{2,1,0:T(8,128)(2,1)}, u32[]{:S(2)}, u32[]{:S(2)}) %all-to-all-start) | async-done | bytes 4194336 | tf_op jit(solution)/shard_map/all_to_all | solution.py:75
  175.9 3.1 multiply_reduce_fusion
  181.3 20.9 %all-to-all-start.1 = ((bf16[64,4,256]{2,1,0:T(4,128)(2,1)}), bf16[64,4,256]{2,1,0:T(4,128)(2,1)S(1)}, u32[]{:S(2)}, u32[]{:S(2)}) async-start(bf16[64,4,256]{2,1,0:T(4,128)(2,1)} %broadcast_select_fusion), calls=%async_computation.1 | async-start | bytes 262144 | tf_op jit(solution)/shard_map/all_to_all | solution.py:24
  205.6 4.8 %all-to-all-done.1 = bf16[64,4,256]{2,1,0:T(4,128)(2,1)S(1)} async-done(((bf16[64,4,256]{2,1,0:T(4,128)(2,1)}), bf16[64,4,256]{2,1,0:T(4,128)(2,1)S(1)}, u32[]{:S(2)}, u32[]{:S(2)}) %all-to-all-start.1) | async-done | bytes 131104 | tf_op jit(solution)/shard_map/all_to_all | solution.py:24
  219.2 5.3 %fusion.7 = bf16[256,256]{1,0:T(8,128)(2,1)} fusion(bf16[8,256,512]{2,1,0:T(8,128)(2,1)S(1)} %bitcast_dynamic-update-slice_fusion.7, f32[256,8,512]{2,0,1:T(8,128)} %copy-done.2, bf16[8,512,256]{2,1,0:T(8,128)(2,1)} %bitcast_dynamic-update-slice_fusion, bf16[256,256]{1,0:T(8,128)(2,1)S(1)} %get-tuple-element.37), kind=kOutput, calls=%fused_computation.25 | convolution fusion | flops 1084162048 | bytes 8650752 | tf_op jit(solution)/shard_map/rkf,kef->kre/dot_general | solution.py:138
  227.6 9.1 %all-to-all-start.3 = ((f32[64,4,384]{2,1,0:T(4,128)}), f32[64,4,384]{2,1,0:T(4,128)S(1)}, u32[]{:S(2)}, u32[]{:S(2)}) async-start(f32[64,4,384]{2,1,0:T(4,128)} %concatenate.23), calls=%async_computation.3 | async-start | bytes 786432 | tf_op jit(solution)/shard_map/all_to_all | solution.py:24
  236.7 11.9 %all-to-all-done.3 = f32[64,4,384]{2,1,0:T(4,128)S(1)} async-done(((f32[64,4,384]{2,1,0:T(4,128)}), f32[64,4,384]{2,1,0:T(4,128)S(1)}, u32[]{:S(2)}, u32[]{:S(2)}) %all-to-all-start.3) | async-done | bytes 393248 | tf_op jit(solution)/shard_map/all_to_all | solution.py:24
  249.8 3.4 multiply_convert_fusion
  253.3 9.3 %all-to-all-start.4 = ((bf16[64,128,256]{2,1,0:T(8,128)(2,1)}), bf16[64,128,256]{2,1,0:T(8,128)(2,1)}, u32[]{:S(2)}, u32[]{:S(2)}) async-start(bf16[64,128,256]{2,1,0:T(8,128)(2,1)} %multiply_convert_fusion), calls=%async_computation.4 | async-start | bytes 8388608 | tf_op jit(solution)/shard_map/all_to_all | solution.py:158
  262.7 3.0 collective-permute-start.15
  265.6 6.1 %collective-permute-start.16 = (bf16[256,256]{1,0:T(8,128)(2,1)S(1)}, bf16[256,256]{1,0:T(8,128)(2,1)S(1)}, u32[]{:S(2)}, u32[]{:S(2)}) collective-permute-start(bf16[256,256]{1,0:T(8,128)(2,1)S(1)} %copy-done.7), channel_id=1, source_target_pairs={{0,3},{1,4},{2,5},{3,6},{4,7},{5,0},{6,1},{7,2},{8,11},{9,12},{10,... | collective-permute-start | bytes 393224 | tf_op jit(solution)/shard_map/ppermute | solution.py:33
  274.0 4.9 %collective-permute-start.18 = (bf16[256,256]{1,0:T(8,128)(2,1)S(1)}, bf16[256,256]{1,0:T(8,128)(2,1)S(1)}, u32[]{:S(2)}, u32[]{:S(2)}) collective-permute-start(bf16[256,256]{1,0:T(8,128)(2,1)S(1)} %copy-done.7), channel_id=1, source_target_pairs={{0,5},{1,6},{2,7},{3,0},{4,1},{5,2},{6,3},{7,4},{8,13},{9,14},{10,... | collective-permute-start | bytes 393224 | tf_op jit(solution)/shard_map/ppermute | solution.py:33
  279.0 4.5 %collective-permute-start.19 = (bf16[256,256]{1,0:T(8,128)(2,1)S(1)}, bf16[256,256]{1,0:T(8,128)(2,1)S(1)}, u32[]{:S(2)}, u32[]{:S(2)}) collective-permute-start(bf16[256,256]{1,0:T(8,128)(2,1)S(1)} %copy-done.7), channel_id=1, source_target_pairs={{0,6},{1,7},{2,0},{3,1},{4,2},{5,3},{6,4},{7,5},{8,14},{9,15},{10,... | collective-permute-start | bytes 393224 | tf_op jit(solution)/shard_map/ppermute | solution.py:33
  288.6 5.4 %collective-permute-start.24 = (bf16[256,256]{1,0:T(8,128)(2,1)S(1)}, bf16[256,256]{1,0:T(8,128)(2,1)S(1)}, u32[]{:S(2)}, u32[]{:S(2)}) collective-permute-start(bf16[256,256]{1,0:T(8,128)(2,1)S(1)} %copy-done.9), channel_id=1, source_target_pairs={{0,4},{1,5},{2,6},{3,7},{4,0},{5,1},{6,2},{7,3},{8,12},{9,13},{10,... | collective-permute-start | bytes 393224 | tf_op jit(solution)/shard_map/ppermute | solution.py:33
  296.7 3.9 collective-permute-start.26
  309.0 5.2 %fusion.8 = f32[1,256,512]{2,1,0:T(8,128)} fusion(bf16[2048,256]{1,0:T(8,128)(2,1)S(1)} %bitcast.146, f32[2048,512]{1,0:T(8,128)} %fusion.35, bf16[2048,256]{1,0:T(8,128)(2,1)S(1)} %bitcast.169, bf16[1,512,256]{2,1,0:T(8,128)(2,1)} %param.22), kind=kOutput, calls=%fused_computation.26 | convolution fusion | flops 1083179008 | bytes 7077888 | tf_op jit(solution)/shard_map/dot_general | solution.py:185
  314.1 65.0 %all-to-all-done.4 = bf16[64,128,256]{2,1,0:T(8,128)(2,1)} async-done(((bf16[64,128,256]{2,1,0:T(8,128)(2,1)}), bf16[64,128,256]{2,1,0:T(8,128)(2,1)}, u32[]{:S(2)}, u32[]{:S(2)}) %all-to-all-start.4) | async-done | bytes 4194336 | tf_op jit(solution)/shard_map/all_to_all | solution.py:158
  379.1 4.7 %fusion.49 = f32[256,256]{1,0:T(8,128)S(1)} fusion(bf16[256,8192]{1,0:T(8,128)(2,1)} %convert_reduce_fusion, bf16[8192,256]{1,0:T(8,128)(2,1)} %bitcast.43), kind=kOutput, calls=%fused_computation.142 | convolution fusion | flops 1073741824 | bytes 8650752 | tf_op jit(solution)/shard_map/dot_general | solution.py:161
  385.0 13.5 %all-to-all-start.5 = ((f32[8,64,256]{2,1,0:T(8,128)}), f32[8,64,256]{2,1,0:T(8,128)S(1)}, u32[]{:S(2)}, u32[]{:S(2)}) async-start(f32[8,64,256]{2,1,0:T(8,128)} %bitcast.44), calls=%async_computation.5 | async-start | bytes 1048576 | tf_op jit(solution)/shard_map/all_to_all | solution.py:167
  398.6 4.3 %fusion.9 = f32[1,512,256]{2,1,0:T(8,128)} fusion(bf16[2048,256]{1,0:T(8,128)(2,1)S(1)} %bitcast.170, f32[2048,512]{1,0:T(8,128)} %fusion.35), kind=kOutput, calls=%fused_computation.27 | convolution fusion | flops 542113792 | bytes 5767168 | tf_op jit(solution)/shard_map/dot_general | solution.py:182
  403.5 5.4 %all-to-all-done.5 = f32[8,64,256]{2,1,0:T(8,128)S(1)} async-done(((f32[8,64,256]{2,1,0:T(8,128)}), f32[8,64,256]{2,1,0:T(8,128)S(1)}, u32[]{:S(2)}, u32[]{:S(2)}) %all-to-all-start.5) | async-done | bytes 524320 | tf_op jit(solution)/shard_map/all_to_all | solution.py:167
  (169 shorter events, 70.5 us)
Async XLA Ops:
  6.6 37.3 %all-to-all-start.2 = ((f32[64,4,128]{2,1,0:T(4,128)}), f32[64,4,128]{2,1,0:T(4,128)S(1)}, u32[]{:S(2)}, u32[]{:S(2)}) async-start(f32[64,4,128]{2,1,0:T(4,128)} %broadcast_select_fusion.2), calls=%async_computation.2 | async-start | bytes 262144 | tf_op jit(solution)/shard_map/all_to_all | solution.py:24
  43.9 132.0 %all-to-all-start = ((bf16[64,128,256]{2,1,0:T(8,128)(2,1)}), bf16[64,128,256]{2,1,0:T(8,128)(2,1)}, u32[]{:S(2)}, u32[]{:S(2)}) async-start(bf16[64,128,256]{2,1,0:T(8,128)(2,1)} %bitcast.143), calls=%async_computation | async-start | bytes 8388608 | tf_op jit(solution)/shard_map/all_to_all | solution.py:75
  57.0 16.9 %collective-permute-start = (bf16[256,512]{1,0:T(8,128)(2,1)S(1)}, bf16[256,512]{1,0:T(8,128)(2,1)}, u32[]{:S(2)}, u32[]{:S(2)}) collective-permute-start(bf16[256,512]{1,0:T(8,128)(2,1)S(1)} %bitcast.149), channel_id=1, source_target_pairs={{0,1},{1,2},{2,3},{3,4},{4,5},{5,6},{6,7},{7,0},{8,9},{9,10},{10,1... | collective-permute-start | bytes 786440 | tf_op jit(solution)/shard_map/ppermute | solution.py:33
  57.0 21.2 %collective-permute-start.1 = (bf16[256,512]{1,0:T(8,128)(2,1)S(1)}, bf16[256,512]{1,0:T(8,128)(2,1)}, u32[]{:S(2)}, u32[]{:S(2)}) collective-permute-start(bf16[256,512]{1,0:T(8,128)(2,1)S(1)} %bitcast.150), channel_id=1, source_target_pairs={{0,2},{1,3},{2,4},{3,5},{4,6},{5,7},{6,0},{7,1},{8,10},{9,11},{10,... | collective-permute-start | bytes 786440 | tf_op jit(solution)/shard_map/ppermute | solution.py:33
  60.4 18.8 %collective-permute-start.2 = (bf16[256,512]{1,0:T(8,128)(2,1)S(1)}, bf16[256,512]{1,0:T(8,128)(2,1)}, u32[]{:S(2)}, u32[]{:S(2)}) collective-permute-start(bf16[256,512]{1,0:T(8,128)(2,1)S(1)} %bitcast.151), channel_id=1, source_target_pairs={{0,3},{1,4},{2,5},{3,6},{4,7},{5,0},{6,1},{7,2},{8,11},{9,12},{10,... | collective-permute-start | bytes 786440 | tf_op jit(solution)/shard_map/ppermute | solution.py:33
  64.4 17.2 %collective-permute-start.3 = (bf16[256,512]{1,0:T(8,128)(2,1)S(1)}, bf16[256,512]{1,0:T(8,128)(2,1)}, u32[]{:S(2)}, u32[]{:S(2)}) collective-permute-start(bf16[256,512]{1,0:T(8,128)(2,1)S(1)} %bitcast.152), channel_id=1, source_target_pairs={{0,4},{1,5},{2,6},{3,7},{4,0},{5,1},{6,2},{7,3},{8,12},{9,13},{10,... | collective-permute-start | bytes 786440 | tf_op jit(solution)/shard_map/ppermute | solution.py:33
  68.4 16.1 %collective-permute-start.4 = (bf16[256,512]{1,0:T(8,128)(2,1)S(1)}, bf16[256,512]{1,0:T(8,128)(2,1)S(1)}, u32[]{:S(2)}, u32[]{:S(2)}) collective-permute-start(bf16[256,512]{1,0:T(8,128)(2,1)S(1)} %bitcast.153), channel_id=1, source_target_pairs={{0,5},{1,6},{2,7},{3,0},{4,1},{5,2},{6,3},{7,4},{8,13},{9,14},{10,... | collective-permute-start | bytes 786440 | tf_op jit(solution)/shard_map/ppermute | solution.py:33
  73.9 13.5 %collective-permute-start.5 = (bf16[256,512]{1,0:T(8,128)(2,1)S(1)}, bf16[256,512]{1,0:T(8,128)(2,1)S(1)}, u32[]{:S(2)}, u32[]{:S(2)}) collective-permute-start(bf16[256,512]{1,0:T(8,128)(2,1)S(1)} %bitcast.154), channel_id=1, source_target_pairs={{0,6},{1,7},{2,0},{3,1},{4,2},{5,3},{6,4},{7,5},{8,14},{9,15},{10,... | collective-permute-start | bytes 786440 | tf_op jit(solution)/shard_map/ppermute | solution.py:33
  78.2 15.0 %collective-permute-start.6 = (bf16[256,512]{1,0:T(8,128)(2,1)S(1)}, bf16[256,512]{1,0:T(8,128)(2,1)S(1)}, u32[]{:S(2)}, u32[]{:S(2)}) collective-permute-start(bf16[256,512]{1,0:T(8,128)(2,1)S(1)} %bitcast.155), channel_id=1, source_target_pairs={{0,7},{1,0},{2,1},{3,2},{4,3},{5,4},{6,5},{7,6},{8,15},{9,8},{10,9... | collective-permute-start | bytes 786440 | tf_op jit(solution)/shard_map/ppermute | solution.py:33
  79.2 16.2 %collective-permute-start.7 = (bf16[512,256]{1,0:T(8,128)(2,1)}, bf16[512,256]{1,0:T(8,128)(2,1)S(1)}, u32[]{:S(2)}, u32[]{:S(2)}) collective-permute-start(bf16[512,256]{1,0:T(8,128)(2,1)} %bitcast.20), channel_id=1, source_target_pairs={{0,1},{1,2},{2,3},{3,4},{4,5},{5,6},{6,7},{7,0},{8,9},{9,10},{10,1... | collective-permute-start | bytes 786440 | tf_op jit(solution)/shard_map/ppermute | solution.py:33
  81.6 18.0 %collective-permute-start.8 = (bf16[512,256]{1,0:T(8,128)(2,1)}, bf16[512,256]{1,0:T(8,128)(2,1)S(1)}, u32[]{:S(2)}, u32[]{:S(2)}) collective-permute-start(bf16[512,256]{1,0:T(8,128)(2,1)} %bitcast.20), channel_id=1, source_target_pairs={{0,2},{1,3},{2,4},{3,5},{4,6},{5,7},{6,0},{7,1},{8,10},{9,11},{10,... | collective-permute-start | bytes 786440 | tf_op jit(solution)/shard_map/ppermute | solution.py:33
  84.5 17.1 %collective-permute-start.9 = (bf16[512,256]{1,0:T(8,128)(2,1)}, bf16[512,256]{1,0:T(8,128)(2,1)S(1)}, u32[]{:S(2)}, u32[]{:S(2)}) collective-permute-start(bf16[512,256]{1,0:T(8,128)(2,1)} %bitcast.20), channel_id=1, source_target_pairs={{0,3},{1,4},{2,5},{3,6},{4,7},{5,0},{6,1},{7,2},{8,11},{9,12},{10,... | collective-permute-start | bytes 786440 | tf_op jit(solution)/shard_map/ppermute | solution.py:33
  87.3 16.9 %collective-permute-start.10 = (bf16[512,256]{1,0:T(8,128)(2,1)}, bf16[512,256]{1,0:T(8,128)(2,1)S(1)}, u32[]{:S(2)}, u32[]{:S(2)}) collective-permute-start(bf16[512,256]{1,0:T(8,128)(2,1)} %bitcast.20), channel_id=1, source_target_pairs={{0,4},{1,5},{2,6},{3,7},{4,0},{5,1},{6,2},{7,3},{8,12},{9,13},{10,... | collective-permute-start | bytes 786440 | tf_op jit(solution)/shard_map/ppermute | solution.py:33
  93.2 11.8 %collective-permute-start.11 = (bf16[512,256]{1,0:T(8,128)(2,1)}, bf16[512,256]{1,0:T(8,128)(2,1)S(1)}, u32[]{:S(2)}, u32[]{:S(2)}) collective-permute-start(bf16[512,256]{1,0:T(8,128)(2,1)} %bitcast.20), channel_id=1, source_target_pairs={{0,5},{1,6},{2,7},{3,0},{4,1},{5,2},{6,3},{7,4},{8,13},{9,14},{10,... | collective-permute-start | bytes 786440 | tf_op jit(solution)/shard_map/ppermute | solution.py:33
  95.4 106.8 %collective-permute-start.12 = (bf16[512,256]{1,0:T(8,128)(2,1)}, bf16[512,256]{1,0:T(8,128)(2,1)}, u32[]{:S(2)}, u32[]{:S(2)}) collective-permute-start(bf16[512,256]{1,0:T(8,128)(2,1)} %bitcast.20), channel_id=1, source_target_pairs={{0,6},{1,7},{2,0},{3,1},{4,2},{5,3},{6,4},{7,5},{8,14},{9,15},{10,... | collective-permute-start | bytes 786440 | tf_op jit(solution)/shard_map/ppermute | solution.py:33
  99.6 104.2 %collective-permute-start.13 = (bf16[512,256]{1,0:T(8,128)(2,1)}, bf16[512,256]{1,0:T(8,128)(2,1)}, u32[]{:S(2)}, u32[]{:S(2)}) collective-permute-start(bf16[512,256]{1,0:T(8,128)(2,1)} %bitcast.20), channel_id=1, source_target_pairs={{0,7},{1,0},{2,1},{3,2},{4,3},{5,4},{6,5},{7,6},{8,15},{9,8},{10,9... | collective-permute-start | bytes 786440 | tf_op jit(solution)/shard_map/ppermute | solution.py:33
  181.3 29.0 %all-to-all-start.1 = ((bf16[64,4,256]{2,1,0:T(4,128)(2,1)}), bf16[64,4,256]{2,1,0:T(4,128)(2,1)S(1)}, u32[]{:S(2)}, u32[]{:S(2)}) async-start(bf16[64,4,256]{2,1,0:T(4,128)(2,1)} %broadcast_select_fusion), calls=%async_computation.1 | async-start | bytes 262144 | tf_op jit(solution)/shard_map/all_to_all | solution.py:24
  227.6 21.0 %all-to-all-start.3 = ((f32[64,4,384]{2,1,0:T(4,128)}), f32[64,4,384]{2,1,0:T(4,128)S(1)}, u32[]{:S(2)}, u32[]{:S(2)}) async-start(f32[64,4,384]{2,1,0:T(4,128)} %concatenate.23), calls=%async_computation.3 | async-start | bytes 786432 | tf_op jit(solution)/shard_map/all_to_all | solution.py:24
  253.3 125.8 %all-to-all-start.4 = ((bf16[64,128,256]{2,1,0:T(8,128)(2,1)}), bf16[64,128,256]{2,1,0:T(8,128)(2,1)}, u32[]{:S(2)}, u32[]{:S(2)}) async-start(bf16[64,128,256]{2,1,0:T(8,128)(2,1)} %multiply_convert_fusion), calls=%async_computation.4 | async-start | bytes 8388608 | tf_op jit(solution)/shard_map/all_to_all | solution.py:158
  262.6 16.3 %collective-permute-start.14 = (bf16[256,256]{1,0:T(8,128)(2,1)S(1)}, bf16[256,256]{1,0:T(8,128)(2,1)S(1)}, u32[]{:S(2)}, u32[]{:S(2)}) collective-permute-start(bf16[256,256]{1,0:T(8,128)(2,1)S(1)} %copy-done.7), channel_id=1, source_target_pairs={{0,1},{1,2},{2,3},{3,4},{4,5},{5,6},{6,7},{7,0},{8,9},{9,10},{10,1... | collective-permute-start | bytes 393224 | tf_op jit(solution)/shard_map/ppermute | solution.py:33
  262.7 20.8 %collective-permute-start.15 = (bf16[256,256]{1,0:T(8,128)(2,1)S(1)}, bf16[256,256]{1,0:T(8,128)(2,1)S(1)}, u32[]{:S(2)}, u32[]{:S(2)}) collective-permute-start(bf16[256,256]{1,0:T(8,128)(2,1)S(1)} %copy-done.7), channel_id=1, source_target_pairs={{0,2},{1,3},{2,4},{3,5},{4,6},{5,7},{6,0},{7,1},{8,10},{9,11},{10,... | collective-permute-start | bytes 393224 | tf_op jit(solution)/shard_map/ppermute | solution.py:33
  265.6 17.9 %collective-permute-start.16 = (bf16[256,256]{1,0:T(8,128)(2,1)S(1)}, bf16[256,256]{1,0:T(8,128)(2,1)S(1)}, u32[]{:S(2)}, u32[]{:S(2)}) collective-permute-start(bf16[256,256]{1,0:T(8,128)(2,1)S(1)} %copy-done.7), channel_id=1, source_target_pairs={{0,3},{1,4},{2,5},{3,6},{4,7},{5,0},{6,1},{7,2},{8,11},{9,12},{10,... | collective-permute-start | bytes 393224 | tf_op jit(solution)/shard_map/ppermute | solution.py:33
  271.7 12.4 %collective-permute-start.17 = (bf16[256,256]{1,0:T(8,128)(2,1)S(1)}, bf16[256,256]{1,0:T(8,128)(2,1)S(1)}, u32[]{:S(2)}, u32[]{:S(2)}) collective-permute-start(bf16[256,256]{1,0:T(8,128)(2,1)S(1)} %copy-done.7), channel_id=1, source_target_pairs={{0,4},{1,5},{2,6},{3,7},{4,0},{5,1},{6,2},{7,3},{8,12},{9,13},{10,... | collective-permute-start | bytes 393224 | tf_op jit(solution)/shard_map/ppermute | solution.py:33
  274.0 12.0 %collective-permute-start.18 = (bf16[256,256]{1,0:T(8,128)(2,1)S(1)}, bf16[256,256]{1,0:T(8,128)(2,1)S(1)}, u32[]{:S(2)}, u32[]{:S(2)}) collective-permute-start(bf16[256,256]{1,0:T(8,128)(2,1)S(1)} %copy-done.7), channel_id=1, source_target_pairs={{0,5},{1,6},{2,7},{3,0},{4,1},{5,2},{6,3},{7,4},{8,13},{9,14},{10,... | collective-permute-start | bytes 393224 | tf_op jit(solution)/shard_map/ppermute | solution.py:33
  279.0 9.6 %collective-permute-start.19 = (bf16[256,256]{1,0:T(8,128)(2,1)S(1)}, bf16[256,256]{1,0:T(8,128)(2,1)S(1)}, u32[]{:S(2)}, u32[]{:S(2)}) collective-permute-start(bf16[256,256]{1,0:T(8,128)(2,1)S(1)} %copy-done.7), channel_id=1, source_target_pairs={{0,6},{1,7},{2,0},{3,1},{4,2},{5,3},{6,4},{7,5},{8,14},{9,15},{10,... | collective-permute-start | bytes 393224 | tf_op jit(solution)/shard_map/ppermute | solution.py:33
  283.5 10.5 %collective-permute-start.20 = (bf16[256,256]{1,0:T(8,128)(2,1)S(1)}, bf16[256,256]{1,0:T(8,128)(2,1)S(1)}, u32[]{:S(2)}, u32[]{:S(2)}) collective-permute-start(bf16[256,256]{1,0:T(8,128)(2,1)S(1)} %copy-done.7), channel_id=1, source_target_pairs={{0,7},{1,0},{2,1},{3,2},{4,3},{5,4},{6,5},{7,6},{8,15},{9,8},{10,9... | collective-permute-start | bytes 393224 | tf_op jit(solution)/shard_map/ppermute | solution.py:33
  283.6 13.1 %collective-permute-start.21 = (bf16[256,256]{1,0:T(8,128)(2,1)S(1)}, bf16[256,256]{1,0:T(8,128)(2,1)S(1)}, u32[]{:S(2)}, u32[]{:S(2)}) collective-permute-start(bf16[256,256]{1,0:T(8,128)(2,1)S(1)} %copy-done.9), channel_id=1, source_target_pairs={{0,1},{1,2},{2,3},{3,4},{4,5},{5,6},{6,7},{7,0},{8,9},{9,10},{10,1... | collective-permute-start | bytes 393224 | tf_op jit(solution)/shard_map/ppermute | solution.py:33
  284.1 17.1 %collective-permute-start.22 = (bf16[256,256]{1,0:T(8,128)(2,1)S(1)}, bf16[256,256]{1,0:T(8,128)(2,1)S(1)}, u32[]{:S(2)}, u32[]{:S(2)}) collective-permute-start(bf16[256,256]{1,0:T(8,128)(2,1)S(1)} %copy-done.9), channel_id=1, source_target_pairs={{0,2},{1,3},{2,4},{3,5},{4,6},{5,7},{6,0},{7,1},{8,10},{9,11},{10,... | collective-permute-start | bytes 393224 | tf_op jit(solution)/shard_map/ppermute | solution.py:33
  286.1 15.8 %collective-permute-start.23 = (bf16[256,256]{1,0:T(8,128)(2,1)S(1)}, bf16[256,256]{1,0:T(8,128)(2,1)S(1)}, u32[]{:S(2)}, u32[]{:S(2)}) collective-permute-start(bf16[256,256]{1,0:T(8,128)(2,1)S(1)} %copy-done.9), channel_id=1, source_target_pairs={{0,3},{1,4},{2,5},{3,6},{4,7},{5,0},{6,1},{7,2},{8,11},{9,12},{10,... | collective-permute-start | bytes 393224 | tf_op jit(solution)/shard_map/ppermute | solution.py:33
  288.6 13.9 %collective-permute-start.24 = (bf16[256,256]{1,0:T(8,128)(2,1)S(1)}, bf16[256,256]{1,0:T(8,128)(2,1)S(1)}, u32[]{:S(2)}, u32[]{:S(2)}) collective-permute-start(bf16[256,256]{1,0:T(8,128)(2,1)S(1)} %copy-done.9), channel_id=1, source_target_pairs={{0,4},{1,5},{2,6},{3,7},{4,0},{5,1},{6,2},{7,3},{8,12},{9,13},{10,... | collective-permute-start | bytes 393224 | tf_op jit(solution)/shard_map/ppermute | solution.py:33
  294.0 9.2 %collective-permute-start.25 = (bf16[256,256]{1,0:T(8,128)(2,1)S(1)}, bf16[256,256]{1,0:T(8,128)(2,1)S(1)}, u32[]{:S(2)}, u32[]{:S(2)}) collective-permute-start(bf16[256,256]{1,0:T(8,128)(2,1)S(1)} %copy-done.9), channel_id=1, source_target_pairs={{0,5},{1,6},{2,7},{3,0},{4,1},{5,2},{6,3},{7,4},{8,13},{9,14},{10,... | collective-permute-start | bytes 393224 | tf_op jit(solution)/shard_map/ppermute | solution.py:33
  385.0 23.9 %all-to-all-start.5 = ((f32[8,64,256]{2,1,0:T(8,128)}), f32[8,64,256]{2,1,0:T(8,128)S(1)}, u32[]{:S(2)}, u32[]{:S(2)}) async-start(f32[8,64,256]{2,1,0:T(8,128)} %bitcast.44), calls=%async_computation.5 | async-start | bytes 1048576 | tf_op jit(solution)/shard_map/all_to_all | solution.py:167
  (18 other events, 629.7 us)
